TPU v7x, 128 devices: a whole 4x4x4 slice. The times are simulated.
128 devices in a mesh: grp: 8 (over x, core), blk: 16 (over y, z).
Axes of the slice: x: 4, y: 4, z: 4, core: 2. Of those that a mesh axis runs over, the one named last changes fastest.
Arguments:
- features: bfloat16 [8, 16, 4096, 256], P('grp', 'blk'), may hold values from -6 to 6
- hub_rows: int32 [8, 16, 32], P('grp', 'blk'), may hold values from 0 to 4095
- hub_adjacency: bfloat16 [8, 16, 4096, 512], P('grp', 'blk'), as said below
- tile_row: int32 [8, 16, 160], P('grp', 'blk'), may hold values from 0 to 31
- tile_col: int32 [8, 16, 160], P('grp', 'blk'), may hold values from 0 to 63
- tile_count: int32 [8, 16], P('grp', 'blk'), may hold values from 26 to 160, as said below
- tile_values: bfloat16 [8, 16, 160, 128, 128], P('grp', 'blk'), may hold values from 0 to 0.049804688
- send_rows: int32 [8, 16, 8, 16, 32], P('grp', 'blk'), may hold values from 0 to 4095
- weight: bfloat16 [256, 256], replicated, may hold values from -0.375 to 0.375
Outputs:
- activations: bfloat16 [8, 16, 4096, 256], P('grp', 'blk')
Inputs may be any that keep to these rules, and one draw needn't show every extreme that they name: `tile_count`: some device has exactly 160 live tile slots in every draw. `hub_adjacency`: Non-negative edge weights.
All inputs are finite; a program needn't handle non-finite values.
Results may differ from a plain program's by a relative error of at most 0.0014.
The roundings to bfloat16 on the way count: a program that leaves them out, or rounds other values in their place, can miss the bound.
Values may be sent and summed in bfloat16 or wider, within the bound.
No kernel may reach another device: no remote copies, remote signals or barrier semaphores. Data moves between devices by JAX's collectives and lax.ppermute only.
A program may use at most 128 MiB of HBM per device.

v0:
```python
import functools

import jax
import jax.numpy as jnp
from jax import lax
from jax.experimental import pallas as pl
from jax.experimental.pallas import tpu as pltpu
from jax.sharding import PartitionSpec as P

TB = 128
SLOTS_PER_STEP = 8


def _tile_body(s, rows_ref, cols_ref, count_ref, table_ref, vals_ref, acc_ref, lo):
    width = table_ref.shape[0] // TB
    count = count_ref[0]
    for j in range(SLOTS_PER_STEP):
        t = s * SLOTS_PER_STEP + j
        c = cols_ref[t] - lo
        live = (t < count) & (c >= 0) & (c < width)

        @pl.when(live)
        def _():
            r0 = pl.multiple_of(rows_ref[t] * TB, TB)
            c0 = pl.multiple_of(c * TB, TB)
            acc_ref[pl.ds(r0, TB), :] += jnp.dot(
                vals_ref[j], table_ref[pl.ds(c0, TB), :], preferred_element_type=jnp.float32
            )


def _local_kernel(rows_ref, cols_ref, count_ref, table_ref, vals_ref, adj_ref, hub_ref, acc_ref):
    n = acc_ref.shape[0]
    blk = 512

    @pl.when(pl.program_id(0) == 0)
    def _():
        for i in range(n // blk):
            sl = pl.ds(i * blk, blk)
            acc_ref[sl, :] = jnp.dot(adj_ref[sl, :], hub_ref[...], preferred_element_type=jnp.float32)

    _tile_body(pl.program_id(0), rows_ref, cols_ref, count_ref, table_ref, vals_ref, acc_ref, 0)


def _remote_kernel(rows_ref, cols_ref, count_ref, table_ref, vals_ref, part_ref, w_ref, out_ref,
                   acc_ref, *, lo, tile_steps):
    s = pl.program_id(0)
    blk = out_ref.shape[0]

    @pl.when(s == 0)
    def _():
        acc_ref[...] = jnp.zeros_like(acc_ref)

    @pl.when(s < tile_steps)
    def _():
        _tile_body(s, rows_ref, cols_ref, count_ref, table_ref, vals_ref, acc_ref, lo)

    @pl.when(s >= tile_steps)
    def _():
        r0 = pl.multiple_of((s - tile_steps) * blk, blk)
        agg = (acc_ref[pl.ds(r0, blk), :] + part_ref[...]).astype(jnp.bfloat16)
        mixed = jnp.dot(agg, w_ref[...], preferred_element_type=jnp.float32)
        out_ref[...] = jnp.maximum(mixed, 0.0).astype(out_ref.dtype)


def _vals_map(s, rows, cols, count):
    last = jnp.maximum(count[0] - 1, 0) // SLOTS_PER_STEP
    return (jnp.minimum(s, last), 0, 0)


def local_tiles(rows, cols, count, table, vals, adj, hub):
    n, width = table.shape
    slots = vals.shape[0]
    steps = slots // SLOTS_PER_STEP
    const = lambda s, r, c, k: (0, 0)
    return pl.pallas_call(
        _local_kernel,
        grid_spec=pltpu.PrefetchScalarGridSpec(
            num_scalar_prefetch=3,
            grid=(steps,),
            in_specs=[
                pl.BlockSpec((n, width), const),
                pl.BlockSpec((SLOTS_PER_STEP, TB, TB), _vals_map),
                pl.BlockSpec(adj.shape, const),
                pl.BlockSpec(hub.shape, const),
            ],
            out_specs=pl.BlockSpec((n, width), const),
        ),
        out_shape=jax.ShapeDtypeStruct((n, width), jnp.float32),
    )(rows, cols, count, table, vals, adj, hub)


def remote_tiles(rows, cols, count, table, vals, part, weight, lo):
    n, width = part.shape
    slots = vals.shape[0]
    tile_steps = slots // SLOTS_PER_STEP
    blk = 512
    fin_steps = n // blk
    const = lambda s, r, c, k: (0, 0)
    fin = lambda s, r, c, k: (jnp.maximum(s - tile_steps, 0), 0)
    return pl.pallas_call(
        functools.partial(_remote_kernel, lo=lo, tile_steps=tile_steps),
        grid_spec=pltpu.PrefetchScalarGridSpec(
            num_scalar_prefetch=3,
            grid=(tile_steps + fin_steps,),
            in_specs=[
                pl.BlockSpec(table.shape, const),
                pl.BlockSpec((SLOTS_PER_STEP, TB, TB), _vals_map),
                pl.BlockSpec((blk, width), fin),
                pl.BlockSpec(weight.shape, const),
            ],
            out_specs=pl.BlockSpec((blk, width), fin),
            scratch_shapes=[pltpu.VMEM((n, width), jnp.float32)],
        ),
        out_shape=jax.ShapeDtypeStruct((n, width), jnp.bfloat16),
    )(rows, cols, count, table, vals, part, weight)


def per_device(
    features,
    hub_rows,
    hub_adjacency,
    tile_row,
    tile_col,
    tile_count,
    tile_values,
    send_rows,
    weight,
):
    local = features[0, 0]
    rows = local.shape[0]
    adjacency = hub_adjacency[0, 0]
    hub_block = local[hub_rows[0, 0]]
    n_blk = lax.axis_size("blk")
    copies = jnp.broadcast_to(hub_block[None], (n_blk,) + hub_block.shape)
    hub_group = lax.all_to_all(copies, "blk", split_axis=0, concat_axis=0, tiled=True)
    hub_group = hub_group.reshape(-1, hub_block.shape[-1])
    listing = send_rows[0, 0]
    outgoing = local[listing.reshape(-1)]
    incoming = lax.all_to_all(outgoing, ("grp", "blk"), split_axis=0, concat_axis=0, tiled=True)
    t_rows = tile_row[0, 0]
    t_cols = tile_col[0, 0]
    count = tile_count[0, 0].reshape(1)
    vals = tile_values[0, 0]
    part = local_tiles(t_rows, t_cols, count, local, vals, adjacency, hub_group)
    out = remote_tiles(t_rows, t_cols, count, incoming, vals, part, weight, rows // TB)
    return out[None, None]


def solution(mesh):
    return jax.shard_map(
        per_device,
        mesh=mesh,
        in_specs=(
            P("grp", "blk", None, None),
            P("grp", "blk", None),
            P("grp", "blk", None, None),
            P("grp", "blk", None),
            P("grp", "blk", None),
            P("grp", "blk"),
            P("grp", "blk", None, None, None),
            P("grp", "blk", None, None, None),
            P(),
        ),
        out_specs=P("grp", "blk", None, None),
        check_vma=False,
    )
```

profile of v0, /device:TPU:1, one launch (start us, length us, event | category | flops | bytes accessed | tf_op | source)
XLA Modules:
  0.0 99.1 jit_solution(5259810114814298905)
XLA Ops:
  0.0 0.7 fusion
  0.7 2.5 %gather_fusion.1 = bf16[32,256]{1,0:T(8,128)(2,1)S(1)} fusion(bf16[4096,256]{1,0:T(8,128)(2,1)} %bitcast.19, s32[1024]{0:T(1024)S(1)} %pad_clamp_fusion), kind=kCustom, calls=%fused_computation.1 | custom fusion | bytes 32896 | tf_op jit(solution)/shard_map/gather | solution.py:132
  3.1 0.7 broadcast_in_dim.4
  3.9 8.6 %all-to-all-start.1 = ((bf16[16,32,256]{2,1,0:T(8,128)(2,1)}), bf16[16,32,256]{2,1,0:T(8,128)(2,1)S(1)}, u32[]{:S(2)}, u32[]{:S(2)}) async-start(bf16[16,32,256]{2,1,0:T(8,128)(2,1)} %broadcast_in_dim.4), calls=%async_computation.1 | async-start | bytes 524288 | tf_op jit(solution)/shard_map/all_to_all | solution.py:135
  12.5 0.9 reshape_squeeze.7
  13.4 17.8 %gather_fusion = bf16[4096,256]{1,0:T(8,128)(2,1)} fusion(bf16[4096,256]{1,0:T(8,128)(2,1)} %bitcast.20, s32[4096]{0:T(1024)S(1)} %broadcast_clamp_fusion), kind=kCustom, calls=%fused_computation | custom fusion | bytes 4210688 | tf_op jit(solution)/shard_map/gather | solution.py:138
  31.2 0.0 all-to-all-done.1
  31.2 0.0 copy-start.1
  31.3 0.7 copy-done.1
  31.9 10.1 %all-to-all-start = ((bf16[128,32,256]{2,1,0:T(8,128)(2,1)}), bf16[128,32,256]{2,1,0:T(8,128)(2,1)S(1)}, u32[]{:S(2)}, u32[]{:S(2)}) async-start(bf16[128,32,256]{2,1,0:T(8,128)(2,1)} %bitcast.25), calls=%async_computation | async-start | bytes 4194304 | tf_op jit(solution)/shard_map/all_to_all | solution.py:139
  42.7 22.5 %shard_map.91.part_ref = f32[4096,256]{1,0:T(8,128)} custom-call(s32[160]{0:T(256)} %bitcast.29, s32[160]{0:T(256)} %bitcast.31, s32[1]{0:T(128)} %bitcast.17.count_ref, bf16[4096,256]{1,0:T(8,128)(2,1)} %bitcast.21, bf16[160,128,128]{2,1,0:T(8,128)(2,1)} %bitcast.22, bf16[4096,512]{1,0:T(8,128)(2,1)} %bitcast.26, bf16[512,256]{1,0:T(8,128)(2,1)} %bitcast.27), custom_call_target="tpu_custom_call" | custom-call | tf_op jit(solution)/shard_map/pallas_call | solution.py:75
  65.2 6.4 %all-to-all-done = bf16[128,32,256]{2,1,0:T(8,128)(2,1)S(1)} async-done(((bf16[128,32,256]{2,1,0:T(8,128)(2,1)}), bf16[128,32,256]{2,1,0:T(8,128)(2,1)S(1)}, u32[]{:S(2)}, u32[]{:S(2)}) %all-to-all-start) | async-done | bytes 2097184 | tf_op jit(solution)/shard_map/all_to_all | solution.py:139
  71.6 0.0 copy-start
  71.6 1.3 %copy-done = bf16[128,32,256]{2,1,0:T(8,128)(2,1)} copy-done((bf16[128,32,256]{2,1,0:T(8,128)(2,1)}, bf16[128,32,256]{2,1,0:T(8,128)(2,1)S(1)}, u32[]{:S(2)}) %copy-start) | copy-done | bytes 2097176
  72.9 26.2 %shard_map.92 = bf16[4096,256]{1,0:T(8,128)(2,1)} custom-call(s32[160]{0:T(256)} %bitcast.30, s32[160]{0:T(256)} %bitcast.32, s32[1]{0:T(128)} %bitcast.18.count_ref, bf16[4096,256]{1,0:T(8,128)(2,1)} %bitcast.24, bf16[160,128,128]{2,1,0:T(8,128)(2,1)} %bitcast.23, f32[4096,256]{1,0:T(8,128)} %shard_map.91.part_ref, bf16[256,256]{1,0:T(8,128)(2,1)} %w_ref.1), custom_call_target="tpu_custom_call" | custom-call | tf_op jit(solution)/shard_map/pallas_call | solution.py:100
  (3 shorter events, 0.0 us)
Async XLA Ops:
  3.9 27.4 %all-to-all-start.1 = ((bf16[16,32,256]{2,1,0:T(8,128)(2,1)}), bf16[16,32,256]{2,1,0:T(8,128)(2,1)S(1)}, u32[]{:S(2)}, u32[]{:S(2)}) async-start(bf16[16,32,256]{2,1,0:T(8,128)(2,1)} %broadcast_in_dim.4), calls=%async_computation.1 | async-start | bytes 524288 | tf_op jit(solution)/shard_map/all_to_all | solution.py:135
  31.2 0.7 copy-start.1
  31.9 39.6 %all-to-all-start = ((bf16[128,32,256]{2,1,0:T(8,128)(2,1)}), bf16[128,32,256]{2,1,0:T(8,128)(2,1)S(1)}, u32[]{:S(2)}, u32[]{:S(2)}) async-start(bf16[128,32,256]{2,1,0:T(8,128)(2,1)} %bitcast.25), calls=%async_computation | async-start | bytes 4194304 | tf_op jit(solution)/shard_map/all_to_all | solution.py:139
  71.6 1.3 %copy-start = (bf16[128,32,256]{2,1,0:T(8,128)(2,1)}, bf16[128,32,256]{2,1,0:T(8,128)(2,1)S(1)}, u32[]{:S(2)}) copy-start(bf16[128,32,256]{2,1,0:T(8,128)(2,1)S(1)} %all-to-all-done) | copy-start | bytes 6291460
where the time goes:
time: 100 us; the launch traced here: 99.1 us
  Pallas kernels  48.7 us (49%)
  local copies, waits for them, and re-layouts  23.9 us (24%)
  starting transfers between devices  18.7 us (19%)
  waiting for transfers between devices  6.35 us (6%)
    pallas_call x1, Pallas kernels, remote_tiles(): pl.pallas_call(functools.partial(_remote_kernel, lo=lo, tile_steps=tile_s...  26.2 us
    pallas_call x1, Pallas kernels, local_tiles(): pl.pallas_call(_local_kernel, grid_spec=pltpu.PrefetchScalarGridSpec(num_...  22.5 us
    gather x1, local copies, waits for them, and re-layouts, per_device(): outgoing = local[listing.reshape(-1)]  17.8 us
    all_to_all x1, starting transfers between devices, per_device(): lax.all_to_all(outgoing, ('grp', 'blk'), split_axis=0, concat_axis=0, til...  10.1 us
    all_to_all x1, starting transfers between devices, per_device(): lax.all_to_all(copies, 'blk', split_axis=0, concat_axis=0, tiled=True)  8.6 us
    all_to_all x1, waiting for transfers between devices, per_device(): lax.all_to_all(outgoing, ('grp', 'blk'), split_axis=0, concat_axis=0, til...  6.35 us
    gather x1, local copies, waits for them, and re-layouts, per_device(): hub_block = local[hub_rows[0, 0]]  2.46 us
    unnamed x4, local copies, waits for them, and re-layouts  2.01 us
  transfers between devices with their start and end apart: 2, of which 1 were waited for; matrix products, arithmetic and copies ran while one was open for 19% of the time, Pallas kernels for 23%

commit v1 on v0

v1 whole, which is shorter than its diff:
```python
import functools

import jax
import jax.numpy as jnp
from jax import lax
from jax.experimental import pallas as pl
from jax.experimental.pallas import tpu as pltpu
from jax.sharding import PartitionSpec as P

TB = 128


GROUP = 8


def _slot_loop(order_ref, rows_ref, cols_ref, start, n, table_ref, vals_ref, acc_ref, lo):
    width = table_ref.shape[0] // TB

    def body(g, carry):
        for j in range(GROUP):
            p = g * GROUP + j
            t = order_ref[start + jnp.minimum(p, n - 1)]
            c = jnp.clip(cols_ref[t] - lo, 0, width - 1)
            r0 = pl.multiple_of(rows_ref[t] * TB, TB)
            c0 = pl.multiple_of(c * TB, TB)
            prod = jnp.dot(vals_ref[t], table_ref[pl.ds(c0, TB), :], preferred_element_type=jnp.float32)
            acc_ref[pl.ds(r0, TB), :] += jnp.where(p < n, prod, 0.0)
        return carry

    lax.fori_loop(0, (n + GROUP - 1) // GROUP, body, 0)


def _local_kernel(order_ref, rows_ref, cols_ref, counts_ref, table_ref, vals_ref, adj_ref, hub_ref,
                  acc_ref):
    n = acc_ref.shape[0]
    blk = 512
    for i in range(n // blk):
        sl = pl.ds(i * blk, blk)
        acc_ref[sl, :] = jnp.dot(adj_ref[sl, :], hub_ref[...], preferred_element_type=jnp.float32)
    _slot_loop(order_ref, rows_ref, cols_ref, 0, counts_ref[0], table_ref, vals_ref, acc_ref, 0)


def _remote_kernel(order_ref, rows_ref, cols_ref, counts_ref, table_ref, vals_ref, part_ref, w_ref,
                   out_ref, acc_ref, *, lo):
    s = pl.program_id(0)

    @pl.when(s == 0)
    def _():
        acc_ref[...] = jnp.zeros_like(acc_ref)
        _slot_loop(order_ref, rows_ref, cols_ref, counts_ref[0], counts_ref[1], table_ref, vals_ref,
                   acc_ref, lo)

    @pl.when(s > 0)
    def _():
        blk = out_ref.shape[0]
        r0 = pl.multiple_of((s - 1) * blk, blk)
        agg = (acc_ref[pl.ds(r0, blk), :] + part_ref[...]).astype(jnp.bfloat16)
        mixed = jnp.dot(agg, w_ref[...], preferred_element_type=jnp.float32)
        out_ref[...] = jnp.maximum(mixed, 0.0).astype(out_ref.dtype)


def local_tiles(order, rows, cols, counts, table, vals, adj, hub):
    n, width = table.shape
    const2 = lambda s, *_: (0, 0)
    const3 = lambda s, *_: (0, 0, 0)
    return pl.pallas_call(
        _local_kernel,
        grid_spec=pltpu.PrefetchScalarGridSpec(
            num_scalar_prefetch=4,
            grid=(1,),
            in_specs=[
                pl.BlockSpec((n, width), const2),
                pl.BlockSpec(vals.shape, const3),
                pl.BlockSpec(adj.shape, const2),
                pl.BlockSpec(hub.shape, const2),
            ],
            out_specs=pl.BlockSpec((n, width), const2),
        ),
        out_shape=jax.ShapeDtypeStruct((n, width), jnp.float32),
    )(order, rows, cols, counts, table, vals, adj, hub)


def remote_tiles(order, rows, cols, counts, table, vals, part, weight, lo):
    n, width = part.shape
    blk = 1024
    fin_steps = n // blk
    const2 = lambda s, *_: (0, 0)
    const3 = lambda s, *_: (0, 0, 0)
    fin = lambda s, *_: (jnp.maximum(s - 1, 0), 0)
    return pl.pallas_call(
        functools.partial(_remote_kernel, lo=lo),
        grid_spec=pltpu.PrefetchScalarGridSpec(
            num_scalar_prefetch=4,
            grid=(1 + fin_steps,),
            in_specs=[
                pl.BlockSpec(table.shape, const2),
                pl.BlockSpec(vals.shape, const3),
                pl.BlockSpec((blk, width), fin),
                pl.BlockSpec(weight.shape, const2),
            ],
            out_specs=pl.BlockSpec((blk, width), fin),
            scratch_shapes=[pltpu.VMEM((n, width), jnp.float32)],
        ),
        out_shape=jax.ShapeDtypeStruct((n, width), jnp.bfloat16),
    )(order, rows, cols, counts, table, vals, part, weight)


def slot_order(cols, count, width):
    slots = cols.shape[0]
    t = jnp.arange(slots, dtype=jnp.int32)
    live = t < count
    is_a = live & (cols < width)
    is_b = live & (cols >= width)
    dead = ~live
    n_a = jnp.sum(is_a.astype(jnp.int32))
    n_b = jnp.sum(is_b.astype(jnp.int32))
    pos = jnp.where(
        is_a,
        jnp.cumsum(is_a.astype(jnp.int32)) - 1,
        jnp.where(
            is_b,
            n_a + jnp.cumsum(is_b.astype(jnp.int32)) - 1,
            n_a + n_b + jnp.cumsum(dead.astype(jnp.int32)) - 1,
        ),
    )
    order = jnp.sum(jnp.where(pos[None, :] == t[:, None], t[None, :], 0), axis=1).astype(jnp.int32)
    return order, jnp.stack([n_a, n_b]).astype(jnp.int32)


def per_device(
    features,
    hub_rows,
    hub_adjacency,
    tile_row,
    tile_col,
    tile_count,
    tile_values,
    send_rows,
    weight,
):
    local = features[0, 0]
    rows = local.shape[0]
    adjacency = hub_adjacency[0, 0]
    hub_block = local[hub_rows[0, 0]]
    n_blk = lax.axis_size("blk")
    copies = jnp.broadcast_to(hub_block[None], (n_blk,) + hub_block.shape)
    hub_group = lax.all_to_all(copies, "blk", split_axis=0, concat_axis=0, tiled=True)
    hub_group = hub_group.reshape(-1, hub_block.shape[-1])
    listing = send_rows[0, 0]
    outgoing = local[listing.reshape(-1)]
    incoming = lax.all_to_all(outgoing, ("grp", "blk"), split_axis=0, concat_axis=0, tiled=True)
    t_rows = tile_row[0, 0]
    t_cols = tile_col[0, 0]
    vals = tile_values[0, 0]
    order, counts = slot_order(t_cols, tile_count[0, 0], rows // TB)
    part = local_tiles(order, t_rows, t_cols, counts, local, vals, adjacency, hub_group)
    out = remote_tiles(order, t_rows, t_cols, counts, incoming, vals, part, weight, rows // TB)
    return out[None, None]


def solution(mesh):
    return jax.shard_map(
        per_device,
        mesh=mesh,
        in_specs=(
            P("grp", "blk", None, None),
            P("grp", "blk", None),
            P("grp", "blk", None, None),
            P("grp", "blk", None),
            P("grp", "blk", None),
            P("grp", "blk"),
            P("grp", "blk", None, None, None),
            P("grp", "blk", None, None, None),
            P(),
        ),
        out_specs=P("grp", "blk", None, None),
        check_vma=False,
    )
```

time: 100 us -> 84.7 us (0.85); the launches traced: 99.1 us -> 84.9 us
  Pallas kernels: 48.7 us -> 23.4 us
  other arithmetic: 0.69 us -> 5.81 us
  waiting for transfers between devices: 6.35 us -> 10.5 us
  between operations: 0.7 us -> 2 us
    pallas_call x1, Pallas kernels: 26.2 us -> 12 us  [remote_tiles(): pl.pallas_call(functools.partial(_remote_kernel, lo=lo), grid_spec=pltpu....]
    pallas_call x1, Pallas kernels: 22.5 us -> 11.3 us  [local_tiles(): pl.pallas_call(_local_kernel, grid_spec=pltpu.PrefetchScalarGridSpec(num_...]
    all_to_all x1, waiting for transfers between devices: 6.35 us -> 10.5 us  [per_device(): lax.all_to_all(outgoing, ('grp', 'blk'), split_axis=0, concat_axis=0, til...]
    another operation x0 -> x10, other arithmetic: none -> 3.06 us  [the longest x1 1.87 us: slot_order(): return (order, jnp.stack([n_a, n_b]).astype(jnp.int32))]
    reduce_sum x0 -> x2, other arithmetic: none -> 1.35 us  [the longest x1 0.72 us: slot_order(): n_b = jnp.sum(is_b.astype(jnp.int32))]
    unnamed x4 -> x6, local copies, waits for them, and re-layouts: 2.01 us -> 2.02 us
  transfers between devices with their start and end apart: 2 -> 2, of which waited for: 1 -> 1; matrix products, arithmetic and copies ran while one was open for 19% -> 29% of each run, Pallas kernels for 23% -> 13%
where the time goes in v1:
time: 84.7 us; the launch traced here: 84.9 us
  local copies, waits for them, and re-layouts  24.5 us (29%)
  Pallas kernels  23.4 us (28%)
  starting transfers between devices  18.7 us (22%)
  waiting for transfers between devices  10.5 us (12%)
  other arithmetic  5.81 us (7%)
  between operations  2 us (2%)
    gather x1, local copies, waits for them, and re-layouts, per_device(): outgoing = local[listing.reshape(-1)]  17.8 us
    pallas_call x1, Pallas kernels, remote_tiles(): pl.pallas_call(functools.partial(_remote_kernel, lo=lo), grid_spec=pltpu....  12 us
    pallas_call x1, Pallas kernels, local_tiles(): pl.pallas_call(_local_kernel, grid_spec=pltpu.PrefetchScalarGridSpec(num_...  11.3 us
    all_to_all x1, waiting for transfers between devices, per_device(): lax.all_to_all(outgoing, ('grp', 'blk'), split_axis=0, concat_axis=0, til...  10.5 us
    all_to_all x1, starting transfers between devices, per_device(): lax.all_to_all(outgoing, ('grp', 'blk'), split_axis=0, concat_axis=0, til...  10.1 us
    all_to_all x1, starting transfers between devices, per_device(): lax.all_to_all(copies, 'blk', split_axis=0, concat_axis=0, tiled=True)  8.6 us
    gather x1, local copies, waits for them, and re-layouts, per_device(): hub_block = local[hub_rows[0, 0]]  2.46 us
    unnamed x6, local copies, waits for them, and re-layouts  2.02 us
  transfers between devices with their start and end apart: 2, of which 1 were waited for; matrix products, arithmetic and copies ran while one was open for 29% of the time, Pallas kernels for 13%

profile of v1, /device:TPU:1, one launch (start us, length us, event | category | flops | bytes accessed | tf_op | source)
XLA Modules:
  0.0 84.9 jit_solution(159500465552421733)
XLA Ops:
  0.0 0.7 fusion.2
  0.7 2.5 %gather_fusion.1 = bf16[32,256]{1,0:T(8,128)(2,1)S(1)} fusion(bf16[4096,256]{1,0:T(8,128)(2,1)} %bitcast.33, s32[1024]{0:T(1024)S(1)} %pad_clamp_fusion), kind=kCustom, calls=%fused_computation.1 | custom fusion | bytes 32896 | tf_op jit(solution)/shard_map/gather | solution.py:144
  3.1 0.7 broadcast_in_dim.28
  3.9 8.6 %all-to-all-start.1 = ((bf16[16,32,256]{2,1,0:T(8,128)(2,1)}), bf16[16,32,256]{2,1,0:T(8,128)(2,1)S(1)}, u32[]{:S(2)}, u32[]{:S(2)}) async-start(bf16[16,32,256]{2,1,0:T(8,128)(2,1)} %broadcast_in_dim.28), calls=%async_computation.1 | async-start | bytes 524288 | tf_op jit(solution)/shard_map/all_to_all | solution.py:147
  12.5 0.9 %reshape_squeeze.3 = s32[4096,1]{0,1:T(1,128)S(1)} reshape(s32[1,1,8,16,32]{4,3,2,1,0:T(8,128)} %param.16) | data formatting | bytes 32768 | tf_op jit(solution)/shard_map/reshape;squeeze | solution.py:150
  13.4 17.8 %gather_fusion = bf16[4096,256]{1,0:T(8,128)(2,1)} fusion(bf16[4096,256]{1,0:T(8,128)(2,1)} %bitcast.34, s32[4096]{0:T(1024)S(1)} %broadcast_clamp_fusion), kind=kCustom, calls=%fused_computation | custom fusion | bytes 4210688 | tf_op jit(solution)/shard_map/gather | solution.py:150
  31.2 0.0 all-to-all-done.1
  31.2 0.0 copy-start.1
  31.2 0.0 copy-start.2
  31.2 0.7 copy-done.1
  31.9 10.1 %all-to-all-start = ((bf16[128,32,256]{2,1,0:T(8,128)(2,1)}), bf16[128,32,256]{2,1,0:T(8,128)(2,1)S(1)}, u32[]{:S(2)}, u32[]{:S(2)}) async-start(bf16[128,32,256]{2,1,0:T(8,128)(2,1)} %bitcast.39), calls=%async_computation | async-start | bytes 4194304 | tf_op jit(solution)/shard_map/all_to_all | solution.py:151
  42.7 0.3 reduce-window.37
  43.0 0.1 slice.36
  43.1 0.0 copy-done.2
  43.1 0.7 convert_reduce_fusion
  43.9 0.3 reduce-window.29
  44.2 0.1 slice.33
  44.3 0.3 reduce-window.25
  44.6 0.1 slice.30
  46.0 1.9 %pad_add_fusion.counts_ref = s32[2]{0:T(128)} fusion(s32[1]{0:T(128)} %bitcast.10, s32[1]{0:T(128)} %bitcast.9), kind=kLoop, calls=%fused_computation.24 | loop fusion | flops 2 | bytes 16 | tf_op jit(solution)/shard_map/stack | solution.py:127
  47.9 0.1 slice_reduce_fusion
  48.0 0.1 slice_reduce_fusion.1
  48.1 0.1 slice_reduce_fusion.2
  48.2 0.1 add_bitcast_fusion.2
  48.3 0.1 add_bitcast_fusion
  48.4 0.7 select_select_fusion
  49.1 0.6 select_reduce_fusion.order_ref
  49.7 11.3 %shard_map.91.part_ref = f32[4096,256]{1,0:T(8,128)} custom-call(s32[160]{0:T(256)} %select_reduce_fusion.order_ref, s32[160]{0:T(256)} %bitcast.46, s32[160]{0:T(256)} %bitcast.43, s32[2]{0:T(128)} %pad_add_fusion.counts_ref, bf16[4096,256]{1,0:T(8,128)(2,1)} %bitcast.35, bf16[160,128,128]{2,1,0:T(8,128)(2,1)} %bitcast.36, bf16[4096,512]{1,0:T(8,128)(2,1)} %bitcast.40, ...), custom_call_target="tpu_custom_call" | custom-call | tf_op jit(solution)/shard_map/pallas_call | solution.py:66
  61.0 10.5 %all-to-all-done = bf16[128,32,256]{2,1,0:T(8,128)(2,1)S(1)} async-done(((bf16[128,32,256]{2,1,0:T(8,128)(2,1)}), bf16[128,32,256]{2,1,0:T(8,128)(2,1)S(1)}, u32[]{:S(2)}, u32[]{:S(2)}) %all-to-all-start) | async-done | bytes 2097184 | tf_op jit(solution)/shard_map/all_to_all | solution.py:151
  71.5 0.0 copy-start
  71.5 1.3 %copy-done = bf16[128,32,256]{2,1,0:T(8,128)(2,1)} copy-done((bf16[128,32,256]{2,1,0:T(8,128)(2,1)}, bf16[128,32,256]{2,1,0:T(8,128)(2,1)S(1)}, u32[]{:S(2)}) %copy-start) | copy-done | bytes 2097176
  72.9 12.0 %shard_map.92 = bf16[4096,256]{1,0:T(8,128)(2,1)} custom-call(s32[160]{0:T(256)} %select_reduce_fusion.order_ref, s32[160]{0:T(256)} %bitcast.47, s32[160]{0:T(256)} %bitcast.44, s32[2]{0:T(128)} %pad_add_fusion.counts_ref, bf16[4096,256]{1,0:T(8,128)(2,1)} %bitcast.38, bf16[160,128,128]{2,1,0:T(8,128)(2,1)} %bitcast.37, f32[4096,256]{1,0:T(8,128)} %shard_map.91.part_ref, ...), custom_call_target="tpu_custom_call" | custom-call | tf_op jit(solution)/shard_map/pallas_call | solution.py:90
  (12 shorter events, 0.2 us)
Async XLA Ops:
  3.9 27.4 %all-to-all-start.1 = ((bf16[16,32,256]{2,1,0:T(8,128)(2,1)}), bf16[16,32,256]{2,1,0:T(8,128)(2,1)S(1)}, u32[]{:S(2)}, u32[]{:S(2)}) async-start(bf16[16,32,256]{2,1,0:T(8,128)(2,1)} %broadcast_in_dim.28), calls=%async_computation.1 | async-start | bytes 524288 | tf_op jit(solution)/shard_map/all_to_all | solution.py:147
  31.2 0.7 copy-start.1
  31.2 11.9 %copy-start.2 = (s32[1,1,160]{2,1,0:T(1,128)S(1)}, s32[1,1,160]{2,1,0:T(1,128)}, u32[]{:S(2)}) copy-start(s32[1,1,160]{2,1,0:T(1,128)} %param.13) | copy-start | bytes 1924
  31.9 39.6 %all-to-all-start = ((bf16[128,32,256]{2,1,0:T(8,128)(2,1)}), bf16[128,32,256]{2,1,0:T(8,128)(2,1)S(1)}, u32[]{:S(2)}, u32[]{:S(2)}) async-start(bf16[128,32,256]{2,1,0:T(8,128)(2,1)} %bitcast.39), calls=%async_computation | async-start | bytes 4194304 | tf_op jit(solution)/shard_map/all_to_all | solution.py:151
  71.5 1.3 %copy-start = (bf16[128,32,256]{2,1,0:T(8,128)(2,1)}, bf16[128,32,256]{2,1,0:T(8,128)(2,1)S(1)}, u32[]{:S(2)}) copy-start(bf16[128,32,256]{2,1,0:T(8,128)(2,1)S(1)} %all-to-all-done) | copy-start | bytes 6291460

commit v2 on v1

--- a/solution.py
+++ b/solution.py
@@ -143,11 +143,13 @@
     adjacency = hub_adjacency[0, 0]
     hub_block = local[hub_rows[0, 0]]
     n_blk = lax.axis_size("blk")
-    copies = jnp.broadcast_to(hub_block[None], (n_blk,) + hub_block.shape)
-    hub_group = lax.all_to_all(copies, "blk", split_axis=0, concat_axis=0, tiled=True)
-    hub_group = hub_group.reshape(-1, hub_block.shape[-1])
+    me = lax.axis_index("blk")
+    mine = jnp.arange(n_blk, dtype=jnp.int32)[:, None, None] == me
+    spread = jnp.where(mine, hub_block[None], jnp.zeros_like(hub_block)[None])
+    hub_group = lax.psum(spread, "blk").reshape(-1, hub_block.shape[-1])
     listing = send_rows[0, 0]
     outgoing = local[listing.reshape(-1)]
+    hub_group, outgoing = lax.optimization_barrier((hub_group, outgoing))
     incoming = lax.all_to_all(outgoing, ("grp", "blk"), split_axis=0, concat_axis=0, tiled=True)
     t_rows = tile_row[0, 0]
     t_cols = tile_col[0, 0]

time: 84.7 us -> 155 us (1.83)
  waiting for transfers between devices: 10.5 us -> 79.8 us
  between operations: 2 us -> 15.4 us
  starting transfers between devices: 18.7 us -> 8.82 us
  Pallas kernels: 23.4 us -> 20.3 us
    psum x0 -> x1, waiting for transfers between devices: none -> 67.7 us  [per_device(): hub_group = lax.psum(spread, 'blk').reshape(-1, hub_block.shape[-1])]
    all_to_all x1 -> x0, starting transfers between devices: 8.6 us -> none  [per_device(): lax.all_to_all(copies, 'blk', split_axis=0, concat_axis=0, tiled=True)]
  transfers between devices with their start and end apart: 2 -> 2, of which waited for: 1 -> 2; matrix products, arithmetic and copies ran while one was open for 29% -> 16% of each run, Pallas kernels for 13% -> 6%
where the time goes in v2:
time: 155 us; the launch traced here: 154 us
  waiting for transfers between devices  79.8 us (51%)
  local copies, waits for them, and re-layouts  23.1 us (15%)
  Pallas kernels  20.3 us (13%)
  between operations  15.4 us (10%)
  starting transfers between devices  8.82 us (6%)
  other arithmetic  6.6 us (4%)
    psum x1, waiting for transfers between devices, per_device(): hub_group = lax.psum(spread, 'blk').reshape(-1, hub_block.shape[-1])  67.7 us
    gather x1, local copies, waits for them, and re-layouts, per_device(): outgoing = local[listing.reshape(-1)]  17.8 us
    all_to_all x1, waiting for transfers between devices, per_device(): lax.all_to_all(outgoing, ('grp', 'blk'), split_axis=0, concat_axis=0, til...  12.1 us
    pallas_call x1, Pallas kernels, remote_tiles(): pl.pallas_call(functools.partial(_remote_kernel, lo=lo), grid_spec=pltpu....  10.5 us
    pallas_call x1, Pallas kernels, local_tiles(): pl.pallas_call(_local_kernel, grid_spec=pltpu.PrefetchScalarGridSpec(num_...  9.79 us
    all_to_all x1, starting transfers between devices, per_device(): lax.all_to_all(outgoing, ('grp', 'blk'), split_axis=0, concat_axis=0, til...  8.82 us
  transfers between devices with their start and end apart: 2, of which 2 were waited for; matrix products, arithmetic and copies ran while one was open for 16% of the time, Pallas kernels for 6%

profile of v2, /device:TPU:1, one launch (start us, length us, event | category | flops | bytes accessed | tf_op | source)
XLA Modules:
  0.0 154.0 jit_solution(5084331581446452798)
XLA Ops:
  6.5 0.0 all-reduce.5.cloned.1.call-start
  6.5 0.7 fusion.2
  7.2 2.5 %gather_fusion = bf16[32,256]{1,0:T(8,128)(2,1)S(1)} fusion(bf16[4096,256]{1,0:T(8,128)(2,1)} %bitcast.33, s32[1024]{0:T(1024)S(1)} %pad_clamp_fusion), kind=kCustom, calls=%fused_computation | custom fusion | bytes 32896 | tf_op jit(solution)/shard_map/gather | solution.py:144
  9.7 0.8 broadcast_select_fusion
  10.5 0.0 all-reduce.5.cloned.1.call-update
  10.5 0.9 reshape_squeeze.3
  11.5 17.8 %gather_fusion.1 = bf16[4096,256]{1,0:T(8,128)(2,1)} fusion(bf16[4096,256]{1,0:T(8,128)(2,1)} %bitcast.34, s32[4096]{0:T(1024)S(1)} %broadcast_clamp_fusion), kind=kCustom, calls=%fused_computation.1 | custom fusion | bytes 4210688 | tf_op jit(solution)/shard_map/gather | solution.py:151
  29.3 67.7 %all-reduce.5.cloned.1.call-done.hub_ref = bf16[512,256]{1,0:T(8,128)(2,1)} async-done(((bf16[512,256]{1,0:T(8,128)(2,1)}), bf16[512,256]{1,0:T(8,128)(2,1)}) %all-reduce.5.cloned.1.call-update) | async-done | bytes 262160 | tf_op jit(solution)/shard_map/psum | solution.py:149
  97.0 0.0 copy-start.1
  97.0 8.8 %all-to-all-start = ((bf16[128,32,256]{2,1,0:T(8,128)(2,1)}), bf16[128,32,256]{2,1,0:T(8,128)(2,1)S(1)}, u32[]{:S(2)}, u32[]{:S(2)}) async-start(bf16[128,32,256]{2,1,0:T(8,128)(2,1)} %bitcast.39), calls=%async_computation | async-start | bytes 4194304 | tf_op jit(solution)/shard_map/all_to_all | solution.py:153
  106.5 0.3 reduce-window.37
  106.8 0.1 slice.36
  106.9 0.0 copy-done.1
  106.9 0.7 convert_reduce_fusion
  107.6 0.3 reduce-window.29
  107.9 0.1 slice.33
  108.1 0.3 reduce-window.25
  108.4 0.1 slice.30
  109.8 1.9 %pad_add_fusion.counts_ref = s32[2]{0:T(128)} fusion(s32[1]{0:T(128)} %bitcast.10, s32[1]{0:T(128)} %bitcast.9), kind=kLoop, calls=%fused_computation.25 | loop fusion | flops 2 | bytes 16 | tf_op jit(solution)/shard_map/stack | solution.py:127
  111.6 0.1 slice_reduce_fusion
  111.7 0.1 slice_reduce_fusion.1
  111.9 0.1 slice_reduce_fusion.2
  112.0 0.1 add_bitcast_fusion.2
  112.0 0.1 add_bitcast_fusion
  112.1 0.7 select_select_fusion
  112.8 0.6 select_reduce_fusion.order_ref
  113.5 9.8 %shard_map.91.part_ref = f32[4096,256]{1,0:T(8,128)} custom-call(s32[160]{0:T(256)} %select_reduce_fusion.order_ref, s32[160]{0:T(256)} %bitcast.46, s32[160]{0:T(256)} %bitcast.43, s32[2]{0:T(128)} %pad_add_fusion.counts_ref, bf16[4096,256]{1,0:T(8,128)(2,1)} %bitcast.35, bf16[160,128,128]{2,1,0:T(8,128)(2,1)} %bitcast.36, bf16[4096,512]{1,0:T(8,128)(2,1)} %bitcast.40, ...), custom_call_target="tpu_custom_call" | custom-call | tf_op jit(solution)/shard_map/pallas_call | solution.py:66
  123.2 12.1 %all-to-all-done = bf16[128,32,256]{2,1,0:T(8,128)(2,1)S(1)} async-done(((bf16[128,32,256]{2,1,0:T(8,128)(2,1)}), bf16[128,32,256]{2,1,0:T(8,128)(2,1)S(1)}, u32[]{:S(2)}, u32[]{:S(2)}) %all-to-all-start) | async-done | bytes 2097184 | tf_op jit(solution)/shard_map/all_to_all | solution.py:153
  135.3 0.0 copy-start
  135.3 1.3 copy-done
  136.6 10.5 %shard_map.92 = bf16[4096,256]{1,0:T(8,128)(2,1)} custom-call(s32[160]{0:T(256)} %select_reduce_fusion.order_ref, s32[160]{0:T(256)} %bitcast.47, s32[160]{0:T(256)} %bitcast.44, s32[2]{0:T(128)} %pad_add_fusion.counts_ref, bf16[4096,256]{1,0:T(8,128)(2,1)} %bitcast.38, bf16[160,128,128]{2,1,0:T(8,128)(2,1)} %bitcast.37, f32[4096,256]{1,0:T(8,128)} %shard_map.91.part_ref, ...), custom_call_target="tpu_custom_call" | custom-call | tf_op jit(solution)/shard_map/pallas_call | solution.py:90
  (13 shorter events, 0.2 us)
Async XLA Ops:
  6.5 90.4 %all-reduce.5.cloned.1.call-start = ((), (), s32[]{:S(2)}) async-start(), calls=%async_computation.1 | async-start | bytes 524288 | tf_op jit(solution)/shard_map/psum | solution.py:149
  97.0 9.9 %copy-start.1 = (s32[1,1,160]{2,1,0:T(1,128)S(1)}, s32[1,1,160]{2,1,0:T(1,128)}, u32[]{:S(2)}) copy-start(s32[1,1,160]{2,1,0:T(1,128)} %param.13) | copy-start | bytes 1924
  97.0 38.3 %all-to-all-start = ((bf16[128,32,256]{2,1,0:T(8,128)(2,1)}), bf16[128,32,256]{2,1,0:T(8,128)(2,1)S(1)}, u32[]{:S(2)}, u32[]{:S(2)}) async-start(bf16[128,32,256]{2,1,0:T(8,128)(2,1)} %bitcast.39), calls=%async_computation | async-start | bytes 4194304 | tf_op jit(solution)/shard_map/all_to_all | solution.py:153
  135.3 1.3 copy-start
Sparse Core Ops, SparseCore 0:
  10.6 86.3 all-reduce.4

commit v3 on v1

--- a/solution.py
+++ b/solution.py
@@ -127,6 +127,53 @@
     return order, jnp.stack([n_a, n_b]).astype(jnp.int32)
 
 
+def _gather_kernel(send_ref, hub_idx_ref, feat_ref, out_ref, hub_out_ref, src_ref, dst_ref):
+    n = feat_ref.shape[0]
+    chunk = 512
+    for i in range(n // chunk):
+        sl = pl.ds(i * chunk, chunk)
+        src_ref[sl, :] = feat_ref[sl, :].astype(jnp.float32)
+
+    def body(g, carry):
+        base = pl.multiple_of(g * 8, 8)
+        rows = [src_ref[pl.ds(send_ref[base + k], 1), :] for k in range(8)]
+        dst_ref[pl.ds(base, 8), :] = jnp.concatenate(rows, axis=0)
+        return carry
+
+    lax.fori_loop(0, out_ref.shape[0] // 8, body, 0)
+    for i in range(out_ref.shape[0] // chunk):
+        sl = pl.ds(i * chunk, chunk)
+        out_ref[sl, :] = dst_ref[sl, :].astype(out_ref.dtype)
+    hub = jnp.concatenate(
+        [src_ref[pl.ds(hub_idx_ref[k], 1), :] for k in range(hub_idx_ref.shape[0])], axis=0
+    ).astype(hub_out_ref.dtype)
+    for j in range(hub_out_ref.shape[0]):
+        hub_out_ref[j] = hub
+
+
+def gather_rows(send_idx, hub_idx, feat, copies):
+    n, width = feat.shape
+    m = send_idx.shape[0]
+    h = hub_idx.shape[0]
+    return pl.pallas_call(
+        _gather_kernel,
+        grid_spec=pltpu.PrefetchScalarGridSpec(
+            num_scalar_prefetch=2,
+            grid=(1,),
+            in_specs=[pl.BlockSpec((n, width), lambda s, *_: (0, 0))],
+            out_specs=[
+                pl.BlockSpec((m, width), lambda s, *_: (0, 0)),
+                pl.BlockSpec((copies, h, width), lambda s, *_: (0, 0, 0)),
+            ],
+            scratch_shapes=[pltpu.VMEM((n, width), jnp.float32), pltpu.VMEM((m, width), jnp.float32)],
+        ),
+        out_shape=[
+            jax.ShapeDtypeStruct((m, width), feat.dtype),
+            jax.ShapeDtypeStruct((copies, h, width), feat.dtype),
+        ],
+    )(send_idx, hub_idx, feat)
+
+
 def per_device(
     features,
     hub_rows,
@@ -141,13 +188,11 @@
     local = features[0, 0]
     rows = local.shape[0]
     adjacency = hub_adjacency[0, 0]
-    hub_block = local[hub_rows[0, 0]]
     n_blk = lax.axis_size("blk")
-    copies = jnp.broadcast_to(hub_block[None], (n_blk,) + hub_block.shape)
+    listing = send_rows[0, 0]
+    outgoing, copies = gather_rows(listing.reshape(-1), hub_rows[0, 0], local, n_blk)
     hub_group = lax.all_to_all(copies, "blk", split_axis=0, concat_axis=0, tiled=True)
-    hub_group = hub_group.reshape(-1, hub_block.shape[-1])
-    listing = send_rows[0, 0]
-    outgoing = local[listing.reshape(-1)]
+    hub_group = hub_group.reshape(-1, local.shape[-1])
     incoming = lax.all_to_all(outgoing, ("grp", "blk"), split_axis=0, concat_axis=0, tiled=True)
     t_rows = tile_row[0, 0]
     t_cols = tile_col[0, 0]

time: 84.7 us -> 82 us (0.968); the launches traced: 84.9 us -> 80.9 us
  local copies, waits for them, and re-layouts: 24.5 us -> 3.43 us
  blocking collectives: 0 us -> 16.2 us
  starting transfers between devices: 18.7 us -> 7.59 us
  Pallas kernels: 23.4 us -> 34.3 us
  waiting for transfers between devices: 10.5 us -> 12.4 us
    gather x2 -> x0, local copies, waits for them, and re-layouts: 20.3 us -> none  [the longest x1 17.8 us: per_device(): outgoing = local[listing.reshape(-1)]]
    all_to_all x0 -> x1, blocking collectives: none -> 16.2 us  [per_device(): lax.all_to_all(copies, 'blk', split_axis=0, concat_axis=0, tiled=True)]
    pallas_call x0 -> x1, Pallas kernels: none -> 14.9 us  [gather_rows(): pl.pallas_call(_gather_kernel, grid_spec=pltpu.PrefetchScalarGridSpec(num...]
    all_to_all x1 -> x0, starting transfers between devices: 8.6 us -> none  [per_device(): lax.all_to_all(copies, 'blk', split_axis=0, concat_axis=0, tiled=True)]
    all_to_all x1, starting transfers between devices: 10.1 us -> 7.59 us  [per_device(): lax.all_to_all(outgoing, ('grp', 'blk'), split_axis=0, concat_axis=0, til...]
    pallas_call x1, Pallas kernels: 12 us -> 9.88 us  [remote_tiles(): pl.pallas_call(functools.partial(_remote_kernel, lo=lo), grid_spec=pltpu....]
    pallas_call x1, Pallas kernels: 11.3 us -> 9.48 us  [local_tiles(): pl.pallas_call(_local_kernel, grid_spec=pltpu.PrefetchScalarGridSpec(num_...]
    all_to_all x1, waiting for transfers between devices: 10.5 us -> 12.4 us  [per_device(): lax.all_to_all(outgoing, ('grp', 'blk'), split_axis=0, concat_axis=0, til...]
  transfers between devices with their start and end apart: 2 -> 1, of which waited for: 1 -> 1; matrix products, arithmetic and copies ran while one was open for 29% -> 7% of each run, Pallas kernels for 13% -> 12%
where the time goes in v3:
time: 82 us; the launch traced here: 80.9 us
  Pallas kernels  34.3 us (42%)
  blocking collectives  16.2 us (20%)
  waiting for transfers between devices  12.4 us (15%)
  starting transfers between devices  7.59 us (9%)
  other arithmetic  5.12 us (6%)
  local copies, waits for them, and re-layouts  3.43 us (4%)
  between operations  1.96 us (2%)
    all_to_all x1, blocking collectives, per_device(): lax.all_to_all(copies, 'blk', split_axis=0, concat_axis=0, tiled=True)  16.2 us
    pallas_call x1, Pallas kernels, gather_rows(): pl.pallas_call(_gather_kernel, grid_spec=pltpu.PrefetchScalarGridSpec(num...  14.9 us
    all_to_all x1, waiting for transfers between devices, per_device(): lax.all_to_all(outgoing, ('grp', 'blk'), split_axis=0, concat_axis=0, til...  12.4 us
    pallas_call x1, Pallas kernels, remote_tiles(): pl.pallas_call(functools.partial(_remote_kernel, lo=lo), grid_spec=pltpu....  9.88 us
    pallas_call x1, Pallas kernels, local_tiles(): pl.pallas_call(_local_kernel, grid_spec=pltpu.PrefetchScalarGridSpec(num_...  9.48 us
    all_to_all x1, starting transfers between devices, per_device(): lax.all_to_all(outgoing, ('grp', 'blk'), split_axis=0, concat_axis=0, til...  7.59 us
    another operation x1, other arithmetic, slot_order(): return (order, jnp.stack([n_a, n_b]).astype(jnp.int32))  1.87 us
  transfers between devices with their start and end apart: 1, of which 1 were waited for; matrix products, arithmetic and copies ran while one was open for 7% of the time, Pallas kernels for 12%

profile of v3, /device:TPU:1, one launch (start us, length us, event | category | flops | bytes accessed | tf_op | source)
XLA Modules:
  0.0 80.9 jit_solution(1893675109528089370)
XLA Ops:
  0.0 1.5 %reshape_squeeze.3.send_ref = s32[4096]{0:T(1024)} reshape(s32[1,1,8,16,32]{4,3,2,1,0:T(8,128)} %param.16) | data formatting | bytes 32768 | tf_op jit(solution)/shard_map/reshape;squeeze | solution.py:193
  1.5 14.9 %shard_map.91 = (bf16[4096,256]{1,0:T(8,128)(2,1)}, bf16[16,32,256]{2,1,0:T(8,128)(2,1)}) custom-call(s32[4096]{0:T(1024)} %reshape_squeeze.3.send_ref, s32[32]{0:T(128)} %bitcast.42, bf16[4096,256]{1,0:T(8,128)(2,1)} %bitcast.31), custom_call_target="tpu_custom_call" | custom-call | tf_op jit(solution)/shard_map/pallas_call | solution.py:158
  16.4 16.2 %all_to_all.16 = bf16[16,32,256]{2,1,0:T(8,128)(2,1)} all-to-all(bf16[16,32,256]{2,1,0:T(8,128)(2,1)} %get-tuple-element.8), channel_id=1, replica_groups=mesh['grp'=8,'blk'=16] {'blk'}, dimensions={0} | all-to-all | bytes 524288 | tf_op jit(solution)/shard_map/all_to_all | solution.py:194
  32.6 0.0 copy-start.1
  32.6 7.6 %all-to-all-start = ((bf16[128,32,256]{2,1,0:T(8,128)(2,1)}), bf16[128,32,256]{2,1,0:T(8,128)(2,1)S(1)}, u32[]{:S(2)}, u32[]{:S(2)}) async-start(bf16[128,32,256]{2,1,0:T(8,128)(2,1)} %bitcast.35), calls=%async_computation | async-start | bytes 4194304 | tf_op jit(solution)/shard_map/all_to_all | solution.py:196
  40.9 0.3 reduce-window.37
  41.2 0.1 slice.36
  41.3 0.0 copy-done.1
  41.3 0.7 convert_reduce_fusion
  42.0 0.3 reduce-window.29
  42.3 0.1 slice.33
  42.4 0.3 reduce-window.25
  42.7 0.1 slice.30
  44.1 1.9 %pad_add_fusion.counts_ref = s32[2]{0:T(128)} fusion(s32[1]{0:T(128)} %bitcast.10, s32[1]{0:T(128)} %bitcast.9), kind=kLoop, calls=%fused_computation.17 | loop fusion | flops 2 | bytes 16 | tf_op jit(solution)/shard_map/stack | solution.py:127
  46.0 0.1 slice_reduce_fusion
  46.1 0.1 slice_reduce_fusion.1
  46.2 0.1 slice_reduce_fusion.2
  46.3 0.1 add_bitcast_fusion.2
  46.4 0.1 add_bitcast_fusion
  46.5 0.7 select_select_fusion
  47.2 0.6 select_reduce_fusion.order_ref
  47.8 9.5 %shard_map.92.part_ref = f32[4096,256]{1,0:T(8,128)} custom-call(s32[160]{0:T(256)} %select_reduce_fusion.order_ref, s32[160]{0:T(256)} %bitcast.40, s32[160]{0:T(256)} %bitcast.37, s32[2]{0:T(128)} %pad_add_fusion.counts_ref, bf16[4096,256]{1,0:T(8,128)(2,1)} %bitcast.32, bf16[160,128,128]{2,1,0:T(8,128)(2,1)} %bitcast.29, bf16[4096,512]{1,0:T(8,128)(2,1)} %bitcast.34, ...), custom_call_target="tpu_custom_call" | custom-call | tf_op jit(solution)/shard_map/pallas_call | solution.py:66
  57.3 12.4 %all-to-all-done = bf16[128,32,256]{2,1,0:T(8,128)(2,1)S(1)} async-done(((bf16[128,32,256]{2,1,0:T(8,128)(2,1)}), bf16[128,32,256]{2,1,0:T(8,128)(2,1)S(1)}, u32[]{:S(2)}, u32[]{:S(2)}) %all-to-all-start) | async-done | bytes 2097184 | tf_op jit(solution)/shard_map/all_to_all | solution.py:196
  69.7 0.0 copy-start
  69.7 1.3 %copy-done = bf16[128,32,256]{2,1,0:T(8,128)(2,1)} copy-done((bf16[128,32,256]{2,1,0:T(8,128)(2,1)}, bf16[128,32,256]{2,1,0:T(8,128)(2,1)S(1)}, u32[]{:S(2)}) %copy-start) | copy-done | bytes 2097176
  71.0 9.9 %shard_map.93 = bf16[4096,256]{1,0:T(8,128)(2,1)} custom-call(s32[160]{0:T(256)} %select_reduce_fusion.order_ref, s32[160]{0:T(256)} %bitcast.41, s32[160]{0:T(256)} %bitcast.38, s32[2]{0:T(128)} %pad_add_fusion.counts_ref, bf16[4096,256]{1,0:T(8,128)(2,1)} %bitcast.33, bf16[160,128,128]{2,1,0:T(8,128)(2,1)} %bitcast.30, f32[4096,256]{1,0:T(8,128)} %shard_map.92.part_ref, ...), custom_call_target="tpu_custom_call" | custom-call | tf_op jit(solution)/shard_map/pallas_call | solution.py:90
  (9 shorter events, 0.1 us)
Async XLA Ops:
  32.6 8.7 %copy-start.1 = (s32[1,1,160]{2,1,0:T(1,128)S(1)}, s32[1,1,160]{2,1,0:T(1,128)}, u32[]{:S(2)}) copy-start(s32[1,1,160]{2,1,0:T(1,128)} %param.13) | copy-start | bytes 1924
  32.6 37.1 %all-to-all-start = ((bf16[128,32,256]{2,1,0:T(8,128)(2,1)}), bf16[128,32,256]{2,1,0:T(8,128)(2,1)S(1)}, u32[]{:S(2)}, u32[]{:S(2)}) async-start(bf16[128,32,256]{2,1,0:T(8,128)(2,1)} %bitcast.35), calls=%async_computation | async-start | bytes 4194304 | tf_op jit(solution)/shard_map/all_to_all | solution.py:196
  69.7 1.3 %copy-start = (bf16[128,32,256]{2,1,0:T(8,128)(2,1)}, bf16[128,32,256]{2,1,0:T(8,128)(2,1)S(1)}, u32[]{:S(2)}) copy-start(bf16[128,32,256]{2,1,0:T(8,128)(2,1)S(1)} %all-to-all-done) | copy-start | bytes 6291460

commit v4 on v3

--- a/solution.py
+++ b/solution.py
@@ -189,10 +189,16 @@
     rows = local.shape[0]
     adjacency = hub_adjacency[0, 0]
     n_blk = lax.axis_size("blk")
+    me = lax.axis_index("blk")
+    hub_block = local[hub_rows[0, 0]]
+    shifted = [hub_block] + [
+        lax.ppermute(hub_block, "blk", [(i, (i + k) % n_blk) for i in range(n_blk)])
+        for k in range(1, n_blk)
+    ]
+    stacked = jnp.stack(shifted[::-1], axis=0)
+    hub_group = jnp.roll(stacked, me + 1, axis=0).reshape(-1, local.shape[-1])
     listing = send_rows[0, 0]
-    outgoing, copies = gather_rows(listing.reshape(-1), hub_rows[0, 0], local, n_blk)
-    hub_group = lax.all_to_all(copies, "blk", split_axis=0, concat_axis=0, tiled=True)
-    hub_group = hub_group.reshape(-1, local.shape[-1])
+    outgoing, _ = gather_rows(listing.reshape(-1), hub_rows[0, 0], local, 1)
     incoming = lax.all_to_all(outgoing, ("grp", "blk"), split_axis=0, concat_axis=0, tiled=True)
     t_rows = tile_row[0, 0]
     t_cols = tile_col[0, 0]

time: 82 us -> 146 us (1.78)
  the two profiles are of different devices: /device:TPU:1 before, /device:TPU:12 now
where the time goes in v4:
time: 146 us; the launch traced here: 144 us
  starting transfers between devices  46.8 us (32%)
  waiting for transfers between devices  44.8 us (31%)
  Pallas kernels  38.2 us (26%)
  local copies, waits for them, and re-layouts  6.71 us (5%)
  other arithmetic  5.64 us (4%)
  between operations  2.16 us (1%)
    ppermute x15, waiting for transfers between devices, per_device(): lax.ppermute(hub_block, 'blk', [(i, (i + k) % n_blk) for i in range(n_blk)])  44.8 us
    ppermute x15, starting transfers between devices, per_device(): lax.ppermute(hub_block, 'blk', [(i, (i + k) % n_blk) for i in range(n_blk)])  39 us
    pallas_call x1, Pallas kernels, gather_rows(): pl.pallas_call(_gather_kernel, grid_spec=pltpu.PrefetchScalarGridSpec(num...  14.8 us
    pallas_call x1, Pallas kernels, remote_tiles(): pl.pallas_call(functools.partial(_remote_kernel, lo=lo), grid_spec=pltpu....  12.1 us
    pallas_call x1, Pallas kernels, local_tiles(): pl.pallas_call(_local_kernel, grid_spec=pltpu.PrefetchScalarGridSpec(num_...  11.3 us
    all_to_all x1, starting transfers between devices, per_device(): lax.all_to_all(outgoing, ('grp', 'blk'), split_axis=0, concat_axis=0, til...  7.8 us
  transfers between devices with their start and end apart: 16, of which 10 were waited for; matrix products, arithmetic and copies ran while one was open for 5% of the time, Pallas kernels for 18%

profile of v4, /device:TPU:12, one launch (start us, length us, event | category | flops | bytes accessed | tf_op | source)
XLA Modules:
  0.0 144.3 jit_solution(7005482025600686623)
XLA Ops:
  0.0 0.7 fusion.2
  0.7 2.5 %gather_fusion = bf16[32,256]{1,0:T(8,128)(2,1)S(1)} fusion(bf16[4096,256]{1,0:T(8,128)(2,1)} %bitcast.83, s32[1024]{0:T(1024)S(1)} %pad_clamp_fusion), kind=kCustom, calls=%fused_computation | custom fusion | bytes 32896 | tf_op jit(solution)/shard_map/gather | solution.py:193
  3.1 2.0 %collective-permute-start.14 = (bf16[32,256]{1,0:T(8,128)(2,1)S(1)}, bf16[32,256]{1,0:T(8,128)(2,1)S(1)}, u32[]{:S(2)}, u32[]{:S(2)}) collective-permute-start(bf16[32,256]{1,0:T(8,128)(2,1)S(1)} %gather_fusion), channel_id=1, source_target_pairs={{0,1},{1,2},{2,3},{3,4},{4,5},{5,6},{6,7},{7,8},{8,9},{9,10},{10,1... | collective-permute-start | bytes 49160 | tf_op jit(solution)/shard_map/ppermute | solution.py:195
  5.1 3.6 %collective-permute-start.13 = (bf16[32,256]{1,0:T(8,128)(2,1)S(1)}, bf16[32,256]{1,0:T(8,128)(2,1)S(1)}, u32[]{:S(2)}, u32[]{:S(2)}) collective-permute-start(bf16[32,256]{1,0:T(8,128)(2,1)S(1)} %gather_fusion), channel_id=1, source_target_pairs={{0,2},{1,3},{2,4},{3,5},{4,6},{5,7},{6,8},{7,9},{8,10},{9,11},{10,... | collective-permute-start | bytes 49160 | tf_op jit(solution)/shard_map/ppermute | solution.py:195
  8.7 2.0 %collective-permute-start.12 = (bf16[32,256]{1,0:T(8,128)(2,1)S(1)}, bf16[32,256]{1,0:T(8,128)(2,1)S(1)}, u32[]{:S(2)}, u32[]{:S(2)}) collective-permute-start(bf16[32,256]{1,0:T(8,128)(2,1)S(1)} %gather_fusion), channel_id=1, source_target_pairs={{0,3},{1,4},{2,5},{3,6},{4,7},{5,8},{6,9},{7,10},{8,11},{9,12},{10... | collective-permute-start | bytes 49160 | tf_op jit(solution)/shard_map/ppermute | solution.py:195
  10.7 1.3 collective-permute-start.11
  12.0 0.4 collective-permute-start
  12.4 1.5 %reshape_squeeze.3.send_ref = s32[4096]{0:T(1024)} reshape(s32[1,1,8,16,32]{4,3,2,1,0:T(8,128)} %param.16) | data formatting | bytes 32768 | tf_op jit(solution)/shard_map/reshape;squeeze | solution.py:201
  13.9 14.8 %shard_map.91 = (bf16[4096,256]{1,0:T(8,128)(2,1)}, bf16[1,32,256]{2,1,0:T(8,128)(2,1)}) custom-call(s32[4096]{0:T(1024)} %reshape_squeeze.3.send_ref, s32[32]{0:T(128)} %bitcast.95, bf16[4096,256]{1,0:T(8,128)(2,1)} %bitcast.84), custom_call_target="tpu_custom_call" | custom-call | tf_op jit(solution)/shard_map/pallas_call | solution.py:158
  28.8 0.0 copy-start.1
  28.8 7.8 %all-to-all-start = ((bf16[128,32,256]{2,1,0:T(8,128)(2,1)}), bf16[128,32,256]{2,1,0:T(8,128)(2,1)S(1)}, u32[]{:S(2)}, u32[]{:S(2)}) async-start(bf16[128,32,256]{2,1,0:T(8,128)(2,1)} %bitcast.88), calls=%async_computation | async-start | bytes 4194304 | tf_op jit(solution)/shard_map/all_to_all | solution.py:202
  37.2 0.3 reduce-window.37
  37.5 0.1 slice.36
  37.7 0.1 slice_reduce_fusion
  37.8 0.0 copy-done.1
  37.8 0.7 convert_reduce_fusion
  38.5 0.3 reduce-window.29
  38.8 0.1 slice.33
  38.9 0.1 slice_reduce_fusion.1
  39.1 0.3 reduce-window.25
  39.4 0.1 slice.30
  39.5 0.1 slice_reduce_fusion.2
  39.6 0.1 add_bitcast_fusion.2
  40.9 0.1 add_bitcast_fusion
  41.0 0.6 select_select_fusion
  41.6 0.6 select_reduce_fusion.order_ref
  42.2 1.9 %pad_add_fusion.counts_ref = s32[2]{0:T(128)} fusion(s32[1]{0:T(128)} %bitcast.10, s32[1]{0:T(128)} %bitcast.9), kind=kLoop, calls=%fused_computation.53 | loop fusion | flops 2 | bytes 16 | tf_op jit(solution)/shard_map/stack | solution.py:127
  44.1 0.0 collective-permute-done
  44.1 3.4 %collective-permute-start.1 = (bf16[32,256]{1,0:T(8,128)(2,1)S(1)}, bf16[32,256]{1,0:T(8,128)(2,1)S(1)}, u32[]{:S(2)}, u32[]{:S(2)}) collective-permute-start(bf16[32,256]{1,0:T(8,128)(2,1)S(1)} %gather_fusion), channel_id=1, source_target_pairs={{0,14},{1,15},{2,0},{3,1},{4,2},{5,3},{6,4},{7,5},{8,6},{9,7},{10,... | collective-permute-start | bytes 49160 | tf_op jit(solution)/shard_map/ppermute | solution.py:195
  47.5 10.9 %collective-permute-done.1 = bf16[32,256]{1,0:T(8,128)(2,1)S(1)} collective-permute-done((bf16[32,256]{1,0:T(8,128)(2,1)S(1)}, bf16[32,256]{1,0:T(8,128)(2,1)S(1)}, u32[]{:S(2)}, u32[]{:S(2)}) %collective-permute-start.1) | collective-permute-done | bytes 16416 | tf_op jit(solution)/shard_map/ppermute | solution.py:195
  58.3 2.1 %collective-permute-start.2 = (bf16[32,256]{1,0:T(8,128)(2,1)S(1)}, bf16[32,256]{1,0:T(8,128)(2,1)S(1)}, u32[]{:S(2)}, u32[]{:S(2)}) collective-permute-start(bf16[32,256]{1,0:T(8,128)(2,1)S(1)} %gather_fusion), channel_id=1, source_target_pairs={{0,13},{1,14},{2,15},{3,0},{4,1},{5,2},{6,3},{7,4},{8,5},{9,6},{10... | collective-permute-start | bytes 49160 | tf_op jit(solution)/shard_map/ppermute | solution.py:195
  60.4 6.1 %collective-permute-done.2 = bf16[32,256]{1,0:T(8,128)(2,1)S(1)} collective-permute-done((bf16[32,256]{1,0:T(8,128)(2,1)S(1)}, bf16[32,256]{1,0:T(8,128)(2,1)S(1)}, u32[]{:S(2)}, u32[]{:S(2)}) %collective-permute-start.2) | collective-permute-done | bytes 16416 | tf_op jit(solution)/shard_map/ppermute | solution.py:195
  66.5 1.6 %collective-permute-start.3 = (bf16[32,256]{1,0:T(8,128)(2,1)S(1)}, bf16[32,256]{1,0:T(8,128)(2,1)S(1)}, u32[]{:S(2)}, u32[]{:S(2)}) collective-permute-start(bf16[32,256]{1,0:T(8,128)(2,1)S(1)} %gather_fusion), channel_id=1, source_target_pairs={{0,12},{1,13},{2,14},{3,15},{4,0},{5,1},{6,2},{7,3},{8,4},{9,5},{1... | collective-permute-start | bytes 49160 | tf_op jit(solution)/shard_map/ppermute | solution.py:195
  68.1 3.5 %collective-permute-done.3 = bf16[32,256]{1,0:T(8,128)(2,1)S(1)} collective-permute-done((bf16[32,256]{1,0:T(8,128)(2,1)S(1)}, bf16[32,256]{1,0:T(8,128)(2,1)S(1)}, u32[]{:S(2)}, u32[]{:S(2)}) %collective-permute-start.3) | collective-permute-done | bytes 16416 | tf_op jit(solution)/shard_map/ppermute | solution.py:195
  71.7 4.5 %collective-permute-start.4 = (bf16[32,256]{1,0:T(8,128)(2,1)S(1)}, bf16[32,256]{1,0:T(8,128)(2,1)S(1)}, u32[]{:S(2)}, u32[]{:S(2)}) collective-permute-start(bf16[32,256]{1,0:T(8,128)(2,1)S(1)} %gather_fusion), channel_id=1, source_target_pairs={{0,11},{1,12},{2,13},{3,14},{4,15},{5,0},{6,1},{7,2},{8,3},{9,4},{... | collective-permute-start | bytes 49160 | tf_op jit(solution)/shard_map/ppermute | solution.py:195
  76.2 1.4 collective-permute-done.4
  77.7 3.4 %collective-permute-start.5 = (bf16[32,256]{1,0:T(8,128)(2,1)S(1)}, bf16[32,256]{1,0:T(8,128)(2,1)S(1)}, u32[]{:S(2)}, u32[]{:S(2)}) collective-permute-start(bf16[32,256]{1,0:T(8,128)(2,1)S(1)} %gather_fusion), channel_id=1, source_target_pairs={{0,10},{1,11},{2,12},{3,13},{4,14},{5,15},{6,0},{7,1},{8,2},{9,3},... | collective-permute-start | bytes 49160 | tf_op jit(solution)/shard_map/ppermute | solution.py:195
  81.1 2.7 %collective-permute-done.5 = bf16[32,256]{1,0:T(8,128)(2,1)S(1)} collective-permute-done((bf16[32,256]{1,0:T(8,128)(2,1)S(1)}, bf16[32,256]{1,0:T(8,128)(2,1)S(1)}, u32[]{:S(2)}, u32[]{:S(2)}) %collective-permute-start.5) | collective-permute-done | bytes 16416 | tf_op jit(solution)/shard_map/ppermute | solution.py:195
  83.8 5.7 %collective-permute-start.6 = (bf16[32,256]{1,0:T(8,128)(2,1)S(1)}, bf16[32,256]{1,0:T(8,128)(2,1)S(1)}, u32[]{:S(2)}, u32[]{:S(2)}) collective-permute-start(bf16[32,256]{1,0:T(8,128)(2,1)S(1)} %gather_fusion), channel_id=1, source_target_pairs={{0,9},{1,10},{2,11},{3,12},{4,13},{5,14},{6,15},{7,0},{8,1},{9,2},... | collective-permute-start | bytes 49160 | tf_op jit(solution)/shard_map/ppermute | solution.py:195
  89.5 1.4 collective-permute-done.6
  91.0 4.8 %collective-permute-start.7 = (bf16[32,256]{1,0:T(8,128)(2,1)S(1)}, bf16[32,256]{1,0:T(8,128)(2,1)S(1)}, u32[]{:S(2)}, u32[]{:S(2)}) collective-permute-start(bf16[32,256]{1,0:T(8,128)(2,1)S(1)} %gather_fusion), channel_id=1, source_target_pairs={{0,8},{1,9},{2,10},{3,11},{4,12},{5,13},{6,14},{7,15},{8,0},{9,1},... | collective-permute-start | bytes 49160 | tf_op jit(solution)/shard_map/ppermute | solution.py:195
  95.7 1.7 %collective-permute-done.7 = bf16[32,256]{1,0:T(8,128)(2,1)S(1)} collective-permute-done((bf16[32,256]{1,0:T(8,128)(2,1)S(1)}, bf16[32,256]{1,0:T(8,128)(2,1)S(1)}, u32[]{:S(2)}, u32[]{:S(2)}) %collective-permute-start.7) | collective-permute-done | bytes 16416 | tf_op jit(solution)/shard_map/ppermute | solution.py:195
  97.4 3.0 %collective-permute-start.8 = (bf16[32,256]{1,0:T(8,128)(2,1)S(1)}, bf16[32,256]{1,0:T(8,128)(2,1)S(1)}, u32[]{:S(2)}, u32[]{:S(2)}) collective-permute-start(bf16[32,256]{1,0:T(8,128)(2,1)S(1)} %gather_fusion), channel_id=1, source_target_pairs={{0,7},{1,8},{2,9},{3,10},{4,11},{5,12},{6,13},{7,14},{8,15},{9,0},... | collective-permute-start | bytes 49160 | tf_op jit(solution)/shard_map/ppermute | solution.py:195
  100.4 3.1 %collective-permute-done.8 = bf16[32,256]{1,0:T(8,128)(2,1)S(1)} collective-permute-done((bf16[32,256]{1,0:T(8,128)(2,1)S(1)}, bf16[32,256]{1,0:T(8,128)(2,1)S(1)}, u32[]{:S(2)}, u32[]{:S(2)}) %collective-permute-start.8) | collective-permute-done | bytes 16416 | tf_op jit(solution)/shard_map/ppermute | solution.py:195
  103.6 1.0 collective-permute-start.9
  104.6 6.6 %collective-permute-done.9 = bf16[32,256]{1,0:T(8,128)(2,1)S(1)} collective-permute-done((bf16[32,256]{1,0:T(8,128)(2,1)S(1)}, bf16[32,256]{1,0:T(8,128)(2,1)S(1)}, u32[]{:S(2)}, u32[]{:S(2)}) %collective-permute-start.9) | collective-permute-done | bytes 16416 | tf_op jit(solution)/shard_map/ppermute | solution.py:195
  111.2 0.1 collective-permute-start.10
  111.3 7.3 %collective-permute-done.10 = bf16[32,256]{1,0:T(8,128)(2,1)S(1)} collective-permute-done((bf16[32,256]{1,0:T(8,128)(2,1)S(1)}, bf16[32,256]{1,0:T(8,128)(2,1)S(1)}, u32[]{:S(2)}, u32[]{:S(2)}) %collective-permute-start.10) | collective-permute-done | bytes 16416 | tf_op jit(solution)/shard_map/ppermute | solution.py:195
  118.6 0.0 collective-permute-done.11
  118.6 0.0 collective-permute-done.12
  118.6 0.0 collective-permute-done.13
  118.6 0.0 collective-permute-done.14
  118.9 0.7 constant_dynamic-slice_fusion
  119.6 11.3 %shard_map.92.part_ref = f32[4096,256]{1,0:T(8,128)} custom-call(s32[160]{0:T(256)} %select_reduce_fusion.order_ref, s32[160]{0:T(256)} %bitcast.93, s32[160]{0:T(256)} %bitcast.90, s32[2]{0:T(128)} %pad_add_fusion.counts_ref, bf16[4096,256]{1,0:T(8,128)(2,1)} %bitcast.85, bf16[160,128,128]{2,1,0:T(8,128)(2,1)} %bitcast.81, bf16[4096,512]{1,0:T(8,128)(2,1)} %bitcast.87, ...), custom_call_target="tpu_custom_call" | custom-call | tf_op jit(solution)/shard_map/pallas_call | solution.py:66
  130.9 0.0 all-to-all-done
  130.9 0.0 copy-start
  130.9 1.3 copy-done
  132.2 12.1 %shard_map.93 = bf16[4096,256]{1,0:T(8,128)(2,1)} custom-call(s32[160]{0:T(256)} %select_reduce_fusion.order_ref, s32[160]{0:T(256)} %bitcast.94, s32[160]{0:T(256)} %bitcast.91, s32[2]{0:T(128)} %pad_add_fusion.counts_ref, bf16[4096,256]{1,0:T(8,128)(2,1)} %bitcast.86, bf16[160,128,128]{2,1,0:T(8,128)(2,1)} %bitcast.82, f32[4096,256]{1,0:T(8,128)} %shard_map.92.part_ref, ...), custom_call_target="tpu_custom_call" | custom-call | tf_op jit(solution)/shard_map/pallas_call | solution.py:90
  (42 shorter events, 0.2 us)
Async XLA Ops:
  3.1 115.5 %collective-permute-start.14 = (bf16[32,256]{1,0:T(8,128)(2,1)S(1)}, bf16[32,256]{1,0:T(8,128)(2,1)S(1)}, u32[]{:S(2)}, u32[]{:S(2)}) collective-permute-start(bf16[32,256]{1,0:T(8,128)(2,1)S(1)} %gather_fusion), channel_id=1, source_target_pairs={{0,1},{1,2},{2,3},{3,4},{4,5},{5,6},{6,7},{7,8},{8,9},{9,10},{10,1... | collective-permute-start | bytes 49160 | tf_op jit(solution)/shard_map/ppermute | solution.py:195
  5.1 113.5 %collective-permute-start.13 = (bf16[32,256]{1,0:T(8,128)(2,1)S(1)}, bf16[32,256]{1,0:T(8,128)(2,1)S(1)}, u32[]{:S(2)}, u32[]{:S(2)}) collective-permute-start(bf16[32,256]{1,0:T(8,128)(2,1)S(1)} %gather_fusion), channel_id=1, source_target_pairs={{0,2},{1,3},{2,4},{3,5},{4,6},{5,7},{6,8},{7,9},{8,10},{9,11},{10,... | collective-permute-start | bytes 49160 | tf_op jit(solution)/shard_map/ppermute | solution.py:195
  8.7 109.9 %collective-permute-start.12 = (bf16[32,256]{1,0:T(8,128)(2,1)S(1)}, bf16[32,256]{1,0:T(8,128)(2,1)S(1)}, u32[]{:S(2)}, u32[]{:S(2)}) collective-permute-start(bf16[32,256]{1,0:T(8,128)(2,1)S(1)} %gather_fusion), channel_id=1, source_target_pairs={{0,3},{1,4},{2,5},{3,6},{4,7},{5,8},{6,9},{7,10},{8,11},{9,12},{10... | collective-permute-start | bytes 49160 | tf_op jit(solution)/shard_map/ppermute | solution.py:195
  10.7 107.9 %collective-permute-start.11 = (bf16[32,256]{1,0:T(8,128)(2,1)S(1)}, bf16[32,256]{1,0:T(8,128)(2,1)S(1)}, u32[]{:S(2)}, u32[]{:S(2)}) collective-permute-start(bf16[32,256]{1,0:T(8,128)(2,1)S(1)} %gather_fusion), channel_id=1, source_target_pairs={{0,4},{1,5},{2,6},{3,7},{4,8},{5,9},{6,10},{7,11},{8,12},{9,13},{1... | collective-permute-start | bytes 49160 | tf_op jit(solution)/shard_map/ppermute | solution.py:195
  12.0 32.1 %collective-permute-start = (bf16[32,256]{1,0:T(8,128)(2,1)S(1)}, bf16[32,256]{1,0:T(8,128)(2,1)S(1)}, u32[]{:S(2)}, u32[]{:S(2)}) collective-permute-start(bf16[32,256]{1,0:T(8,128)(2,1)S(1)} %gather_fusion), channel_id=1, source_target_pairs={{0,15},{1,0},{2,1},{3,2},{4,3},{5,4},{6,5},{7,6},{8,7},{9,8},{10,9... | collective-permute-start | bytes 49160 | tf_op jit(solution)/shard_map/ppermute | solution.py:195
  28.8 9.0 %copy-start.1 = (s32[1,1,160]{2,1,0:T(1,128)S(1)}, s32[1,1,160]{2,1,0:T(1,128)}, u32[]{:S(2)}) copy-start(s32[1,1,160]{2,1,0:T(1,128)} %param.13) | copy-start | bytes 1924
  28.8 102.1 %all-to-all-start = ((bf16[128,32,256]{2,1,0:T(8,128)(2,1)}), bf16[128,32,256]{2,1,0:T(8,128)(2,1)S(1)}, u32[]{:S(2)}, u32[]{:S(2)}) async-start(bf16[128,32,256]{2,1,0:T(8,128)(2,1)} %bitcast.88), calls=%async_computation | async-start | bytes 4194304 | tf_op jit(solution)/shard_map/all_to_all | solution.py:202
  44.1 14.3 %collective-permute-start.1 = (bf16[32,256]{1,0:T(8,128)(2,1)S(1)}, bf16[32,256]{1,0:T(8,128)(2,1)S(1)}, u32[]{:S(2)}, u32[]{:S(2)}) collective-permute-start(bf16[32,256]{1,0:T(8,128)(2,1)S(1)} %gather_fusion), channel_id=1, source_target_pairs={{0,14},{1,15},{2,0},{3,1},{4,2},{5,3},{6,4},{7,5},{8,6},{9,7},{10,... | collective-permute-start | bytes 49160 | tf_op jit(solution)/shard_map/ppermute | solution.py:195
  58.3 8.2 %collective-permute-start.2 = (bf16[32,256]{1,0:T(8,128)(2,1)S(1)}, bf16[32,256]{1,0:T(8,128)(2,1)S(1)}, u32[]{:S(2)}, u32[]{:S(2)}) collective-permute-start(bf16[32,256]{1,0:T(8,128)(2,1)S(1)} %gather_fusion), channel_id=1, source_target_pairs={{0,13},{1,14},{2,15},{3,0},{4,1},{5,2},{6,3},{7,4},{8,5},{9,6},{10... | collective-permute-start | bytes 49160 | tf_op jit(solution)/shard_map/ppermute | solution.py:195
  66.5 5.2 %collective-permute-start.3 = (bf16[32,256]{1,0:T(8,128)(2,1)S(1)}, bf16[32,256]{1,0:T(8,128)(2,1)S(1)}, u32[]{:S(2)}, u32[]{:S(2)}) collective-permute-start(bf16[32,256]{1,0:T(8,128)(2,1)S(1)} %gather_fusion), channel_id=1, source_target_pairs={{0,12},{1,13},{2,14},{3,15},{4,0},{5,1},{6,2},{7,3},{8,4},{9,5},{1... | collective-permute-start | bytes 49160 | tf_op jit(solution)/shard_map/ppermute | solution.py:195
  71.7 6.0 %collective-permute-start.4 = (bf16[32,256]{1,0:T(8,128)(2,1)S(1)}, bf16[32,256]{1,0:T(8,128)(2,1)S(1)}, u32[]{:S(2)}, u32[]{:S(2)}) collective-permute-start(bf16[32,256]{1,0:T(8,128)(2,1)S(1)} %gather_fusion), channel_id=1, source_target_pairs={{0,11},{1,12},{2,13},{3,14},{4,15},{5,0},{6,1},{7,2},{8,3},{9,4},{... | collective-permute-start | bytes 49160 | tf_op jit(solution)/shard_map/ppermute | solution.py:195
  77.7 6.1 %collective-permute-start.5 = (bf16[32,256]{1,0:T(8,128)(2,1)S(1)}, bf16[32,256]{1,0:T(8,128)(2,1)S(1)}, u32[]{:S(2)}, u32[]{:S(2)}) collective-permute-start(bf16[32,256]{1,0:T(8,128)(2,1)S(1)} %gather_fusion), channel_id=1, source_target_pairs={{0,10},{1,11},{2,12},{3,13},{4,14},{5,15},{6,0},{7,1},{8,2},{9,3},... | collective-permute-start | bytes 49160 | tf_op jit(solution)/shard_map/ppermute | solution.py:195
  83.8 7.2 %collective-permute-start.6 = (bf16[32,256]{1,0:T(8,128)(2,1)S(1)}, bf16[32,256]{1,0:T(8,128)(2,1)S(1)}, u32[]{:S(2)}, u32[]{:S(2)}) collective-permute-start(bf16[32,256]{1,0:T(8,128)(2,1)S(1)} %gather_fusion), channel_id=1, source_target_pairs={{0,9},{1,10},{2,11},{3,12},{4,13},{5,14},{6,15},{7,0},{8,1},{9,2},... | collective-permute-start | bytes 49160 | tf_op jit(solution)/shard_map/ppermute | solution.py:195
  91.0 6.5 %collective-permute-start.7 = (bf16[32,256]{1,0:T(8,128)(2,1)S(1)}, bf16[32,256]{1,0:T(8,128)(2,1)S(1)}, u32[]{:S(2)}, u32[]{:S(2)}) collective-permute-start(bf16[32,256]{1,0:T(8,128)(2,1)S(1)} %gather_fusion), channel_id=1, source_target_pairs={{0,8},{1,9},{2,10},{3,11},{4,12},{5,13},{6,14},{7,15},{8,0},{9,1},... | collective-permute-start | bytes 49160 | tf_op jit(solution)/shard_map/ppermute | solution.py:195
  97.4 6.1 %collective-permute-start.8 = (bf16[32,256]{1,0:T(8,128)(2,1)S(1)}, bf16[32,256]{1,0:T(8,128)(2,1)S(1)}, u32[]{:S(2)}, u32[]{:S(2)}) collective-permute-start(bf16[32,256]{1,0:T(8,128)(2,1)S(1)} %gather_fusion), channel_id=1, source_target_pairs={{0,7},{1,8},{2,9},{3,10},{4,11},{5,12},{6,13},{7,14},{8,15},{9,0},... | collective-permute-start | bytes 49160 | tf_op jit(solution)/shard_map/ppermute | solution.py:195
  103.6 7.6 %collective-permute-start.9 = (bf16[32,256]{1,0:T(8,128)(2,1)S(1)}, bf16[32,256]{1,0:T(8,128)(2,1)S(1)}, u32[]{:S(2)}, u32[]{:S(2)}) collective-permute-start(bf16[32,256]{1,0:T(8,128)(2,1)S(1)} %gather_fusion), channel_id=1, source_target_pairs={{0,6},{1,7},{2,8},{3,9},{4,10},{5,11},{6,12},{7,13},{8,14},{9,15},... | collective-permute-start | bytes 49160 | tf_op jit(solution)/shard_map/ppermute | solution.py:195
  111.2 7.4 %collective-permute-start.10 = (bf16[32,256]{1,0:T(8,128)(2,1)S(1)}, bf16[32,256]{1,0:T(8,128)(2,1)S(1)}, u32[]{:S(2)}, u32[]{:S(2)}) collective-permute-start(bf16[32,256]{1,0:T(8,128)(2,1)S(1)} %gather_fusion), channel_id=1, source_target_pairs={{0,5},{1,6},{2,7},{3,8},{4,9},{5,10},{6,11},{7,12},{8,13},{9,14},{... | collective-permute-start | bytes 49160 | tf_op jit(solution)/shard_map/ppermute | solution.py:195
  130.9 1.3 copy-start

commit v5 on v3

--- a/solution.py
+++ b/solution.py
@@ -127,7 +127,7 @@
     return order, jnp.stack([n_a, n_b]).astype(jnp.int32)
 
 
-def _gather_kernel(send_ref, hub_idx_ref, feat_ref, out_ref, hub_out_ref, src_ref, dst_ref):
+def _gather_kernel(send_ref, feat_ref, out_ref, src_ref, dst_ref):
     n = feat_ref.shape[0]
     chunk = 512
     for i in range(n // chunk):
@@ -144,34 +144,22 @@
     for i in range(out_ref.shape[0] // chunk):
         sl = pl.ds(i * chunk, chunk)
         out_ref[sl, :] = dst_ref[sl, :].astype(out_ref.dtype)
-    hub = jnp.concatenate(
-        [src_ref[pl.ds(hub_idx_ref[k], 1), :] for k in range(hub_idx_ref.shape[0])], axis=0
-    ).astype(hub_out_ref.dtype)
-    for j in range(hub_out_ref.shape[0]):
-        hub_out_ref[j] = hub
-
-
-def gather_rows(send_idx, hub_idx, feat, copies):
+
+
+def gather_rows(send_idx, feat):
     n, width = feat.shape
     m = send_idx.shape[0]
-    h = hub_idx.shape[0]
     return pl.pallas_call(
         _gather_kernel,
         grid_spec=pltpu.PrefetchScalarGridSpec(
-            num_scalar_prefetch=2,
+            num_scalar_prefetch=1,
             grid=(1,),
             in_specs=[pl.BlockSpec((n, width), lambda s, *_: (0, 0))],
-            out_specs=[
-                pl.BlockSpec((m, width), lambda s, *_: (0, 0)),
-                pl.BlockSpec((copies, h, width), lambda s, *_: (0, 0, 0)),
-            ],
+            out_specs=pl.BlockSpec((m, width), lambda s, *_: (0, 0)),
             scratch_shapes=[pltpu.VMEM((n, width), jnp.float32), pltpu.VMEM((m, width), jnp.float32)],
         ),
-        out_shape=[
-            jax.ShapeDtypeStruct((m, width), feat.dtype),
-            jax.ShapeDtypeStruct((copies, h, width), feat.dtype),
-        ],
-    )(send_idx, hub_idx, feat)
+        out_shape=jax.ShapeDtypeStruct((m, width), feat.dtype),
+    )(send_idx, feat)
 
 
 def per_device(
@@ -189,10 +177,12 @@
     rows = local.shape[0]
     adjacency = hub_adjacency[0, 0]
     n_blk = lax.axis_size("blk")
-    listing = send_rows[0, 0]
-    outgoing, copies = gather_rows(listing.reshape(-1), hub_rows[0, 0], local, n_blk)
+    hub_block = local[hub_rows[0, 0]]
+    copies = jnp.broadcast_to(hub_block[None], (n_blk,) + hub_block.shape)
     hub_group = lax.all_to_all(copies, "blk", split_axis=0, concat_axis=0, tiled=True)
     hub_group = hub_group.reshape(-1, local.shape[-1])
+    listing = send_rows[0, 0]
+    outgoing = gather_rows(listing.reshape(-1), local)
     incoming = lax.all_to_all(outgoing, ("grp", "blk"), split_axis=0, concat_axis=0, tiled=True)
     t_rows = tile_row[0, 0]
     t_cols = tile_col[0, 0]

time: 82 us -> 82.3 us (level)
  the two profiles are of different devices: /device:TPU:1 before, /device:TPU:0 now
where the time goes in v5:
time: 82.3 us
  Pallas kernels  38.2 us (46%)
  starting transfers between devices  18.4 us (22%)
  waiting for transfers between devices  10.7 us (13%)
  local copies, waits for them, and re-layouts  7.3 us (9%)
  other arithmetic  5.79 us (7%)
  between operations  1.97 us (2%)
    pallas_call x1, Pallas kernels, gather_rows(): pl.pallas_call(_gather_kernel, grid_spec=pltpu.PrefetchScalarGridSpec(num...  14.8 us
    pallas_call x1, Pallas kernels, remote_tiles(): pl.pallas_call(functools.partial(_remote_kernel, lo=lo), grid_spec=pltpu....  12 us
    pallas_call x1, Pallas kernels, local_tiles(): pl.pallas_call(_local_kernel, grid_spec=pltpu.PrefetchScalarGridSpec(num_...  11.3 us
    all_to_all x1, waiting for transfers between devices, per_device(): lax.all_to_all(outgoing, ('grp', 'blk'), split_axis=0, concat_axis=0, til...  10.7 us
    all_to_all x1, starting transfers between devices, per_device(): lax.all_to_all(outgoing, ('grp', 'blk'), split_axis=0, concat_axis=0, til...  10.2 us
    all_to_all x1, starting transfers between devices, per_device(): lax.all_to_all(copies, 'blk', split_axis=0, concat_axis=0, tiled=True)  8.13 us
    gather x1, local copies, waits for them, and re-layouts, per_device(): hub_block = local[hub_rows[0, 0]]  2.46 us
    unnamed x6, local copies, waits for them, and re-layouts  2.02 us
  transfers between devices with their start and end apart: 2, of which 1 were waited for; matrix products, arithmetic and copies ran while one was open for 9% of the time, Pallas kernels for 32%

profile of v5, /device:TPU:0, one launch (start us, length us, event | category | flops | bytes accessed | tf_op | source)
XLA Modules:
  0.0 82.3 jit_solution(8497717058964217761)
XLA Ops:
  0.0 0.7 fusion.2
  0.7 2.5 %gather_fusion = bf16[32,256]{1,0:T(8,128)(2,1)S(1)} fusion(bf16[4096,256]{1,0:T(8,128)(2,1)} %bitcast.34, s32[1024]{0:T(1024)S(1)} %pad_clamp_fusion), kind=kCustom, calls=%fused_computation | custom fusion | bytes 32896 | tf_op jit(solution)/shard_map/gather | solution.py:180
  3.1 0.7 broadcast_in_dim.27
  3.9 8.1 %all-to-all-start.1 = ((bf16[16,32,256]{2,1,0:T(8,128)(2,1)}), bf16[16,32,256]{2,1,0:T(8,128)(2,1)S(1)}, u32[]{:S(2)}, u32[]{:S(2)}) async-start(bf16[16,32,256]{2,1,0:T(8,128)(2,1)} %broadcast_in_dim.27), calls=%async_computation.1 | async-start | bytes 524288 | tf_op jit(solution)/shard_map/all_to_all | solution.py:182
  12.0 1.5 %reshape_squeeze.3.send_ref = s32[4096]{0:T(1024)} reshape(s32[1,1,8,16,32]{4,3,2,1,0:T(8,128)} %param.16) | data formatting | bytes 32768 | tf_op jit(solution)/shard_map/reshape;squeeze | solution.py:185
  13.5 14.8 %shard_map.91 = bf16[4096,256]{1,0:T(8,128)(2,1)} custom-call(s32[4096]{0:T(1024)} %reshape_squeeze.3.send_ref, bf16[4096,256]{1,0:T(8,128)(2,1)} %bitcast.35), custom_call_target="tpu_custom_call" | custom-call | tf_op jit(solution)/shard_map/pallas_call | solution.py:152
  28.3 0.0 all-to-all-done.1
  28.3 0.0 copy-start.1
  28.3 0.0 copy-start.2
  28.3 0.7 copy-done.1
  29.0 10.2 %all-to-all-start = ((bf16[128,32,256]{2,1,0:T(8,128)(2,1)}), bf16[128,32,256]{2,1,0:T(8,128)(2,1)S(1)}, u32[]{:S(2)}, u32[]{:S(2)}) async-start(bf16[128,32,256]{2,1,0:T(8,128)(2,1)} %bitcast.38), calls=%async_computation | async-start | bytes 4194304 | tf_op jit(solution)/shard_map/all_to_all | solution.py:186
  39.9 0.3 reduce-window.37
  40.2 0.1 slice.36
  40.3 0.0 copy-done.2
  40.3 0.7 convert_reduce_fusion
  41.1 0.3 reduce-window.29
  41.4 0.1 slice.33
  41.5 0.3 reduce-window.25
  41.8 0.1 slice.30
  43.2 1.9 %pad_add_fusion.counts_ref = s32[2]{0:T(128)} fusion(s32[1]{0:T(128)} %bitcast.10, s32[1]{0:T(128)} %bitcast.9), kind=kLoop, calls=%fused_computation.21 | loop fusion | flops 2 | bytes 16 | tf_op jit(solution)/shard_map/stack | solution.py:127
  45.1 0.1 slice_reduce_fusion
  45.2 0.1 slice_reduce_fusion.1
  45.3 0.1 slice_reduce_fusion.2
  45.4 0.1 add_bitcast_fusion.2
  45.5 0.1 add_bitcast_fusion
  45.6 0.7 select_select_fusion
  46.3 0.6 select_reduce_fusion.order_ref
  46.9 11.3 %shard_map.92.part_ref = f32[4096,256]{1,0:T(8,128)} custom-call(s32[160]{0:T(256)} %select_reduce_fusion.order_ref, s32[160]{0:T(256)} %bitcast.44, s32[160]{0:T(256)} %bitcast.41, s32[2]{0:T(128)} %pad_add_fusion.counts_ref, bf16[4096,256]{1,0:T(8,128)(2,1)} %bitcast.36, bf16[160,128,128]{2,1,0:T(8,128)(2,1)} %bitcast.32, bf16[4096,512]{1,0:T(8,128)(2,1)} %bitcast.39, ...), custom_call_target="tpu_custom_call" | custom-call | tf_op jit(solution)/shard_map/pallas_call | solution.py:66
  58.2 10.7 %all-to-all-done = bf16[128,32,256]{2,1,0:T(8,128)(2,1)S(1)} async-done(((bf16[128,32,256]{2,1,0:T(8,128)(2,1)}), bf16[128,32,256]{2,1,0:T(8,128)(2,1)S(1)}, u32[]{:S(2)}, u32[]{:S(2)}) %all-to-all-start) | async-done | bytes 2097184 | tf_op jit(solution)/shard_map/all_to_all | solution.py:186
  69.0 0.0 copy-start
  69.0 1.3 %copy-done = bf16[128,32,256]{2,1,0:T(8,128)(2,1)} copy-done((bf16[128,32,256]{2,1,0:T(8,128)(2,1)}, bf16[128,32,256]{2,1,0:T(8,128)(2,1)S(1)}, u32[]{:S(2)}) %copy-start) | copy-done | bytes 2097176
  70.3 12.0 %shard_map.93 = bf16[4096,256]{1,0:T(8,128)(2,1)} custom-call(s32[160]{0:T(256)} %select_reduce_fusion.order_ref, s32[160]{0:T(256)} %bitcast.45, s32[160]{0:T(256)} %bitcast.42, s32[2]{0:T(128)} %pad_add_fusion.counts_ref, bf16[4096,256]{1,0:T(8,128)(2,1)} %bitcast.37, bf16[160,128,128]{2,1,0:T(8,128)(2,1)} %bitcast.33, f32[4096,256]{1,0:T(8,128)} %shard_map.92.part_ref, ...), custom_call_target="tpu_custom_call" | custom-call | tf_op jit(solution)/shard_map/pallas_call | solution.py:90
  (10 shorter events, 0.1 us)
Async XLA Ops:
  3.9 24.5 %all-to-all-start.1 = ((bf16[16,32,256]{2,1,0:T(8,128)(2,1)}), bf16[16,32,256]{2,1,0:T(8,128)(2,1)S(1)}, u32[]{:S(2)}, u32[]{:S(2)}) async-start(bf16[16,32,256]{2,1,0:T(8,128)(2,1)} %broadcast_in_dim.27), calls=%async_computation.1 | async-start | bytes 524288 | tf_op jit(solution)/shard_map/all_to_all | solution.py:182
  28.3 0.7 copy-start.1
  28.3 12.0 %copy-start.2 = (s32[1,1,160]{2,1,0:T(1,128)S(1)}, s32[1,1,160]{2,1,0:T(1,128)}, u32[]{:S(2)}) copy-start(s32[1,1,160]{2,1,0:T(1,128)} %param.13) | copy-start | bytes 1924
  29.0 39.9 %all-to-all-start = ((bf16[128,32,256]{2,1,0:T(8,128)(2,1)}), bf16[128,32,256]{2,1,0:T(8,128)(2,1)S(1)}, u32[]{:S(2)}, u32[]{:S(2)}) async-start(bf16[128,32,256]{2,1,0:T(8,128)(2,1)} %bitcast.38), calls=%async_computation | async-start | bytes 4194304 | tf_op jit(solution)/shard_map/all_to_all | solution.py:186
  69.0 1.3 %copy-start = (bf16[128,32,256]{2,1,0:T(8,128)(2,1)}, bf16[128,32,256]{2,1,0:T(8,128)(2,1)S(1)}, u32[]{:S(2)}) copy-start(bf16[128,32,256]{2,1,0:T(8,128)(2,1)S(1)} %all-to-all-done) | copy-start | bytes 6291460

commit v6 on v5

--- a/solution.py
+++ b/solution.py
@@ -135,12 +135,12 @@
         src_ref[sl, :] = feat_ref[sl, :].astype(jnp.float32)
 
     def body(g, carry):
-        base = pl.multiple_of(g * 8, 8)
-        rows = [src_ref[pl.ds(send_ref[base + k], 1), :] for k in range(8)]
-        dst_ref[pl.ds(base, 8), :] = jnp.concatenate(rows, axis=0)
+        base = pl.multiple_of(g * 16, 16)
+        for k in range(16):
+            dst_ref[pl.ds(base + k, 1), :] = src_ref[pl.ds(send_ref[base + k], 1), :]
         return carry
 
-    lax.fori_loop(0, out_ref.shape[0] // 8, body, 0)
+    lax.fori_loop(0, out_ref.shape[0] // 16, body, 0)
     for i in range(out_ref.shape[0] // chunk):
         sl = pl.ds(i * chunk, chunk)
         out_ref[sl, :] = dst_ref[sl, :].astype(out_ref.dtype)

time: 82.3 us -> 86.2 us (1.047)
  the two profiles are of different devices: /device:TPU:0 before, /device:TPU:1 now
where the time goes in v6:
time: 86.2 us; the launch traced here: 85.2 us
  Pallas kernels  41.5 us (48%)
  starting transfers between devices  18.7 us (22%)
  waiting for transfers between devices  9.91 us (11%)
  local copies, waits for them, and re-layouts  7.3 us (8%)
  other arithmetic  5.79 us (7%)
  between operations  1.97 us (2%)
    pallas_call x1, Pallas kernels, gather_rows(): pl.pallas_call(_gather_kernel, grid_spec=pltpu.PrefetchScalarGridSpec(num...  18.2 us
    pallas_call x1, Pallas kernels, local_tiles(): pl.pallas_call(_local_kernel, grid_spec=pltpu.PrefetchScalarGridSpec(num_...  11.9 us
    pallas_call x1, Pallas kernels, remote_tiles(): pl.pallas_call(functools.partial(_remote_kernel, lo=lo), grid_spec=pltpu....  11.4 us
    all_to_all x1, starting transfers between devices, per_device(): lax.all_to_all(outgoing, ('grp', 'blk'), split_axis=0, concat_axis=0, til...  10.1 us
    all_to_all x1, waiting for transfers between devices, per_device(): lax.all_to_all(outgoing, ('grp', 'blk'), split_axis=0, concat_axis=0, til...  9.91 us
    all_to_all x1, starting transfers between devices, per_device(): lax.all_to_all(copies, 'blk', split_axis=0, concat_axis=0, tiled=True)  8.6 us
    gather x1, local copies, waits for them, and re-layouts, per_device(): hub_block = local[hub_rows[0, 0]]  2.46 us
    unnamed x6, local copies, waits for them, and re-layouts  2.02 us
  transfers between devices with their start and end apart: 2, of which 1 were waited for; matrix products, arithmetic and copies ran while one was open for 8% of the time, Pallas kernels for 35%

profile of v6, /device:TPU:1, one launch (start us, length us, event | category | flops | bytes accessed | tf_op | source)
XLA Modules:
  0.0 85.2 jit_solution(614772879954216414)
XLA Ops:
  0.0 0.7 fusion.2
  0.7 2.5 %gather_fusion = bf16[32,256]{1,0:T(8,128)(2,1)S(1)} fusion(bf16[4096,256]{1,0:T(8,128)(2,1)} %bitcast.34, s32[1024]{0:T(1024)S(1)} %pad_clamp_fusion), kind=kCustom, calls=%fused_computation | custom fusion | bytes 32896 | tf_op jit(solution)/shard_map/gather | solution.py:180
  3.1 0.7 broadcast_in_dim.27
  3.9 8.6 %all-to-all-start.1 = ((bf16[16,32,256]{2,1,0:T(8,128)(2,1)}), bf16[16,32,256]{2,1,0:T(8,128)(2,1)S(1)}, u32[]{:S(2)}, u32[]{:S(2)}) async-start(bf16[16,32,256]{2,1,0:T(8,128)(2,1)} %broadcast_in_dim.27), calls=%async_computation.1 | async-start | bytes 524288 | tf_op jit(solution)/shard_map/all_to_all | solution.py:182
  12.5 1.5 %reshape_squeeze.3.send_ref = s32[4096]{0:T(1024)} reshape(s32[1,1,8,16,32]{4,3,2,1,0:T(8,128)} %param.16) | data formatting | bytes 32768 | tf_op jit(solution)/shard_map/reshape;squeeze | solution.py:185
  14.0 18.2 %shard_map.91 = bf16[4096,256]{1,0:T(8,128)(2,1)} custom-call(s32[4096]{0:T(1024)} %reshape_squeeze.3.send_ref, bf16[4096,256]{1,0:T(8,128)(2,1)} %bitcast.35), custom_call_target="tpu_custom_call" | custom-call | tf_op jit(solution)/shard_map/pallas_call | solution.py:152
  32.2 0.0 all-to-all-done.1
  32.2 0.0 copy-start.1
  32.2 0.0 copy-start.2
  32.2 0.7 copy-done.1
  32.8 10.1 %all-to-all-start = ((bf16[128,32,256]{2,1,0:T(8,128)(2,1)}), bf16[128,32,256]{2,1,0:T(8,128)(2,1)S(1)}, u32[]{:S(2)}, u32[]{:S(2)}) async-start(bf16[128,32,256]{2,1,0:T(8,128)(2,1)} %bitcast.38), calls=%async_computation | async-start | bytes 4194304 | tf_op jit(solution)/shard_map/all_to_all | solution.py:186
  43.6 0.3 reduce-window.37
  43.9 0.1 slice.36
  44.1 0.0 copy-done.2
  44.1 0.7 convert_reduce_fusion
  44.8 0.3 reduce-window.29
  45.1 0.1 slice.33
  45.2 0.3 reduce-window.25
  45.5 0.1 slice.30
  46.9 1.9 %pad_add_fusion.counts_ref = s32[2]{0:T(128)} fusion(s32[1]{0:T(128)} %bitcast.10, s32[1]{0:T(128)} %bitcast.9), kind=kLoop, calls=%fused_computation.21 | loop fusion | flops 2 | bytes 16 | tf_op jit(solution)/shard_map/stack | solution.py:127
  48.8 0.1 slice_reduce_fusion
  48.9 0.1 slice_reduce_fusion.1
  49.0 0.1 slice_reduce_fusion.2
  49.1 0.1 add_bitcast_fusion.2
  49.2 0.1 add_bitcast_fusion
  49.3 0.7 select_select_fusion
  50.0 0.6 select_reduce_fusion.order_ref
  50.6 11.9 %shard_map.92.part_ref = f32[4096,256]{1,0:T(8,128)} custom-call(s32[160]{0:T(256)} %select_reduce_fusion.order_ref, s32[160]{0:T(256)} %bitcast.44, s32[160]{0:T(256)} %bitcast.41, s32[2]{0:T(128)} %pad_add_fusion.counts_ref, bf16[4096,256]{1,0:T(8,128)(2,1)} %bitcast.36, bf16[160,128,128]{2,1,0:T(8,128)(2,1)} %bitcast.32, bf16[4096,512]{1,0:T(8,128)(2,1)} %bitcast.39, ...), custom_call_target="tpu_custom_call" | custom-call | tf_op jit(solution)/shard_map/pallas_call | solution.py:66
  62.6 9.9 %all-to-all-done = bf16[128,32,256]{2,1,0:T(8,128)(2,1)S(1)} async-done(((bf16[128,32,256]{2,1,0:T(8,128)(2,1)}), bf16[128,32,256]{2,1,0:T(8,128)(2,1)S(1)}, u32[]{:S(2)}, u32[]{:S(2)}) %all-to-all-start) | async-done | bytes 2097184 | tf_op jit(solution)/shard_map/all_to_all | solution.py:186
  72.5 0.0 copy-start
  72.5 1.3 %copy-done = bf16[128,32,256]{2,1,0:T(8,128)(2,1)} copy-done((bf16[128,32,256]{2,1,0:T(8,128)(2,1)}, bf16[128,32,256]{2,1,0:T(8,128)(2,1)S(1)}, u32[]{:S(2)}) %copy-start) | copy-done | bytes 2097176
  73.8 11.4 %shard_map.93 = bf16[4096,256]{1,0:T(8,128)(2,1)} custom-call(s32[160]{0:T(256)} %select_reduce_fusion.order_ref, s32[160]{0:T(256)} %bitcast.45, s32[160]{0:T(256)} %bitcast.42, s32[2]{0:T(128)} %pad_add_fusion.counts_ref, bf16[4096,256]{1,0:T(8,128)(2,1)} %bitcast.37, bf16[160,128,128]{2,1,0:T(8,128)(2,1)} %bitcast.33, f32[4096,256]{1,0:T(8,128)} %shard_map.92.part_ref, ...), custom_call_target="tpu_custom_call" | custom-call | tf_op jit(solution)/shard_map/pallas_call | solution.py:90
  (10 shorter events, 0.1 us)
Async XLA Ops:
  3.9 28.3 %all-to-all-start.1 = ((bf16[16,32,256]{2,1,0:T(8,128)(2,1)}), bf16[16,32,256]{2,1,0:T(8,128)(2,1)S(1)}, u32[]{:S(2)}, u32[]{:S(2)}) async-start(bf16[16,32,256]{2,1,0:T(8,128)(2,1)} %broadcast_in_dim.27), calls=%async_computation.1 | async-start | bytes 524288 | tf_op jit(solution)/shard_map/all_to_all | solution.py:182
  32.2 0.7 copy-start.1
  32.2 11.9 %copy-start.2 = (s32[1,1,160]{2,1,0:T(1,128)S(1)}, s32[1,1,160]{2,1,0:T(1,128)}, u32[]{:S(2)}) copy-start(s32[1,1,160]{2,1,0:T(1,128)} %param.13) | copy-start | bytes 1924
  32.8 39.6 %all-to-all-start = ((bf16[128,32,256]{2,1,0:T(8,128)(2,1)}), bf16[128,32,256]{2,1,0:T(8,128)(2,1)S(1)}, u32[]{:S(2)}, u32[]{:S(2)}) async-start(bf16[128,32,256]{2,1,0:T(8,128)(2,1)} %bitcast.38), calls=%async_computation | async-start | bytes 4194304 | tf_op jit(solution)/shard_map/all_to_all | solution.py:186
  72.5 1.3 %copy-start = (bf16[128,32,256]{2,1,0:T(8,128)(2,1)}, bf16[128,32,256]{2,1,0:T(8,128)(2,1)S(1)}, u32[]{:S(2)}) copy-start(bf16[128,32,256]{2,1,0:T(8,128)(2,1)S(1)} %all-to-all-done) | copy-start | bytes 6291460
